TPU v7x, 32 devices: a whole 2x2x4 slice. The times are simulated.
32 devices in a mesh: req: 8 (over y, x, core), head: 4 (over z).
Axes of the slice: x: 2, y: 2, z: 4, core: 2. Of those that a mesh axis runs over, the one named last changes fastest.
Arguments:
- tokens: bfloat16 [4096, 2048], P('req'), may hold values from -6 to 6
- norm_gain: float32 [2048], replicated, may hold values from 0.1 to 1.9
- router_weight: float32 [2048, 8], replicated, may hold values from -0.125 to 0.125
- kv_weight: bfloat16 [2048, 4096], P('req', 'head'), may hold values from -0.125 to 0.125
- query_weight: bfloat16 [8, 2048, 2048], P(None, 'req', 'head'), may hold values from -0.125 to 0.125
- out_weight: bfloat16 [8, 2048, 2048], P(None, 'head', 'req'), may hold values from -0.5 to 0.5
- expert_ids: int32 [4096, 2], P('req'), may hold values from 0 to 7, all different within a row
- lengths: int32 [8], replicated, may hold values from 128 to 2048, as said below
- kv_cache: bfloat16 [8, 16, 2048, 256], P('req', 'head'), may hold values from -320 to 320
Outputs:
- attended: bfloat16 [4096, 2048], P(('req', 'head'))
- new_kv: bfloat16 [8, 16, 512, 256], P('req', 'head')
Inputs may be any that keep to these rules, and one draw needn't show every extreme that they name: `lengths`: some request holds exactly 2048 cached positions.
All inputs are finite; a program needn't handle non-finite values.
Results may differ from a plain program's by a relative error of at most 0.012.
The roundings to bfloat16 on the way count: a program that leaves them out, or rounds other values in their place, can miss the bound.
Values may be sent and summed in bfloat16 or wider, within the bound.
No kernel may reach another device: no remote copies, remote signals or barrier semaphores. Data moves between devices by JAX's collectives and lax.ppermute only.
A program may use at most 128 MiB of HBM per device.

v0:
```python
import math

import jax
import jax.numpy as jnp
from jax import lax
from jax.sharding import PartitionSpec as P

NEG_LARGE = -1e30
EPSILON = 1e-06


def normalize(tokens, norm_gain):
    widened = tokens.astype(jnp.float32)
    factor = lax.rsqrt(jnp.mean(widened * widened, axis=-1, keepdims=True) + EPSILON)
    return (widened * factor * norm_gain).astype(jnp.bfloat16)


def gate_pair(normed, router_weight, expert_ids):
    logits = jnp.dot(normed.astype(jnp.float32), router_weight, precision=lax.Precision.HIGHEST)
    one_hot = jnp.arange(router_weight.shape[1])[None, None, :] == expert_ids[:, :, None]
    chosen = jnp.sum(jnp.where(one_hot, logits[:, None, :], 0.0), axis=-1)
    logit_gap = chosen[:, 1] - chosen[:, 0]
    return jnp.stack([1.0 / (1.0 + jnp.exp(logit_gap)), 1.0 / (1.0 + jnp.exp(-logit_gap))], axis=1)


def rotate(vectors, positions):
    half_dim = vectors.shape[-1] // 2
    inv_freq = jnp.exp(-math.log(10000.0) * jnp.arange(half_dim, dtype=jnp.float32) / half_dim)
    angles = positions[:, None] * inv_freq[None, :]
    cosine_table = jnp.cos(angles)
    sine_table = jnp.sin(angles)
    front_half = vectors[..., :half_dim]
    back_half = vectors[..., half_dim:]
    return jnp.concatenate(
        [
            front_half * cosine_table - back_half * sine_table,
            back_half * cosine_table + front_half * sine_table,
        ],
        axis=-1,
    )


def pick_length(lengths, wanted):
    return jnp.sum(jnp.where(jnp.arange(lengths.shape[0]) == wanted, lengths, 0))


def absorb(carry_state, queries, key_rows, value_rows, allowed):
    row_peak, row_total, row_accum = carry_state
    scale_factor = queries.shape[-1] ** (-0.5)
    scores = (
        jnp.einsum("hqd,hkd->hqk", queries, key_rows, preferred_element_type=jnp.float32)
        * scale_factor
    )
    scores = jnp.where(allowed[None], scores, NEG_LARGE)
    new_peak = jnp.maximum(row_peak, jnp.max(scores, axis=-1))
    weights = jnp.where(allowed[None], jnp.exp(scores - new_peak[..., None]), 0.0)
    shrink = jnp.exp(row_peak - new_peak)
    row_total = row_total * shrink + jnp.sum(weights, axis=-1)
    row_accum = row_accum * shrink[..., None] + jnp.einsum(
        "hqk,hkd->hqd", weights.astype(jnp.bfloat16), value_rows, preferred_element_type=jnp.float32
    )
    return (new_peak, row_total, row_accum)


def cache_pass(
    queries, source, lowest, highest, first_block, last_block, anchor, block_len, carry_state
):
    head_dim = source.shape[2] // 2

    def block_step(block_id, running):
        block_rows = lax.dynamic_slice_in_dim(source, block_id * block_len, block_len, 1)
        key_index = anchor + block_id * block_len + jnp.arange(block_len)
        allowed = ((key_index >= lowest) & (key_index < highest))[None, :]
        return absorb(
            running, queries, block_rows[..., :head_dim], block_rows[..., head_dim:], allowed
        )

    return lax.fori_loop(
        jnp.asarray(first_block, jnp.int32),
        jnp.asarray(last_block, jnp.int32),
        block_step,
        carry_state,
    )


def chain_reduce(parts, axis):
    count = lax.axis_size(axis)
    me = lax.axis_index(axis)
    blocks = parts.reshape(count, parts.shape[0] // count, parts.shape[1])
    own = lax.dynamic_index_in_dim(blocks, me, 0, keepdims=False).astype(jnp.float32)
    if count == 1:
        return own.astype(parts.dtype)

    def run(step_block, pairs_of):
        received = None
        for step in range(1, count):
            block = lax.dynamic_index_in_dim(
                blocks, jnp.clip(step_block(step), 0, count - 1), 0, keepdims=False
            )
            if received is not None:
                block = (received.astype(jnp.float32) + block.astype(jnp.float32)).astype(
                    parts.dtype
                )
            received = lax.ppermute(block, axis, pairs_of(step))
        return received.astype(jnp.float32)

    rightward = run(
        lambda step: me + count - step,
        lambda step: [(src, src + 1) for src in range(step) if src + 1 < count],
    )
    leftward = run(
        lambda step: me - count + step,
        lambda step: [(src, src - 1) for src in range(count - step, count) if src >= 1],
    )
    return (own + rightward + leftward).astype(parts.dtype)


def shards(
    tokens,
    norm_gain,
    router_weight,
    kv_weight,
    query_weight,
    out_weight,
    expert_ids,
    lengths,
    kv_cache,
):
    normed = normalize(tokens, norm_gain)
    tok_count = normed.shape[0]
    experts = query_weight.shape[0]
    head_dim = kv_cache.shape[3] // 2
    local_heads = query_weight.shape[2] // head_dim
    cache_len = kv_cache.shape[2]
    block_len = min(512, cache_len // 4)
    gate_values = gate_pair(normed, router_weight, expert_ids)
    query_full = lax.all_gather(query_weight, "req", axis=1, tiled=True)
    query_full, kv_weight, out_weight = lax.optimization_barrier(
        (query_full, kv_weight, out_weight)
    )
    kv_full = lax.all_gather(kv_weight, "req", axis=0, tiled=True)
    out_full = lax.all_gather(out_weight, "req", axis=2, tiled=True)
    projected = jnp.dot(normed, kv_full, preferred_element_type=jnp.float32)
    query_all = jnp.einsum(
        "tc,ecn->ten", normed, query_full, preferred_element_type=jnp.float32
    )
    req_index = lax.axis_index("req")
    own_length = pick_length(lengths, req_index)
    positions = (own_length + jnp.arange(tok_count)).astype(jnp.float32)
    projected = projected.reshape(tok_count, local_heads, 2, head_dim)
    new_keys = rotate(jnp.transpose(projected[:, :, 0], (1, 0, 2)), positions)
    new_values = jnp.transpose(projected[:, :, 1], (1, 0, 2))
    fresh_kv = jnp.concatenate([new_keys, new_values], axis=-1).astype(jnp.bfloat16)
    one_hot = jnp.arange(experts)[None, None, :] == expert_ids[:, :, None]
    query_sel = jnp.sum(jnp.where(one_hot[..., None], query_all[:, None], 0.0), axis=2)
    queries = jnp.transpose(query_sel.reshape(tok_count * 2, local_heads, head_dim), (1, 0, 2))
    queries = rotate(queries, jnp.repeat(positions, 2)).astype(jnp.bfloat16)
    own_cache = kv_cache[0]
    query_rows = tok_count * 2
    empty_state = (
        jnp.full((local_heads, query_rows), NEG_LARGE, jnp.float32),
        jnp.zeros((local_heads, query_rows), jnp.float32),
        jnp.zeros((local_heads, query_rows, head_dim), jnp.float32),
    )
    carry_state = cache_pass(
        queries,
        own_cache,
        0,
        own_length,
        0,
        (own_length + block_len - 1) // block_len,
        0,
        block_len,
        empty_state,
    )
    row_ids = jnp.arange(query_rows) // 2
    causal = row_ids[:, None] >= jnp.arange(tok_count)[None, :]
    carry_state = absorb(
        carry_state, queries, fresh_kv[..., :head_dim], fresh_kv[..., head_dim:], causal
    )
    heads_out = carry_state[2] / carry_state[1][..., None]
    heads_out = jnp.transpose(heads_out, (1, 0, 2)).reshape(tok_count, 2, local_heads * head_dim)
    weighted = (gate_values[:, :, None] * heads_out).astype(jnp.bfloat16)
    mixture = jnp.sum(jnp.where(one_hot[..., None], weighted[:, :, None, :], 0), axis=1)
    mixture_flat = mixture.reshape(tok_count, experts * local_heads * head_dim)
    weight_piece = out_full
    flat_piece = weight_piece.reshape(experts * local_heads * head_dim, weight_piece.shape[2])
    partial_value = jnp.dot(mixture_flat, flat_piece, preferred_element_type=jnp.float32)
    result = chain_reduce(partial_value.astype(jnp.bfloat16), "head")
    return (result, fresh_kv[None])


def solution(mesh):
    placed = (
        P("req", None),
        P(),
        P(),
        P("req", "head"),
        P(None, "req", "head"),
        P(None, "head", "req"),
        P("req", None),
        P(),
        P("req", "head", None, None),
    )
    return jax.shard_map(
        shards,
        mesh=mesh,
        in_specs=placed,
        out_specs=(P(("req", "head"), None), P("req", "head", None, None)),
        check_vma=False,
    )
```

profile of v0, /device:TPU:0, one launch (start us, length us, event | category | flops | bytes accessed | tf_op | source)
XLA Modules:
  0.0 321.2 jit_solution(10567473420410704609)
XLA Ops:
  8.0 94.6 %all-gather.4.cloned.1.call-done = bf16[8,2048,512]{2,1,0:T(8,128)(2,1)} async-done(((bf16[8,256,512]{2,1,0:T(8,128)(2,1)}), bf16[8,2048,512]{2,1,0:T(8,128)(2,1)}) %all-gather.4.cloned.1.call-update) | async-done | bytes 16777232 | tf_op jit(solution)/shard_map/all_gather | solution.py:137
  109.5 2.0 multiply_cosine_fusion.1
  114.5 11.9 %fusion.34 = f32[512,8,512]{2,0,1:T(8,128)S(1)} fusion(bf16[8,2048,512]{2,1,0:T(8,128)(2,1)} %all-gather.4.cloned.1.call-done, bf16[512,2048]{1,0:T(8,128)(2,1)S(1)} %copy-done.5, f32[2048]{0:T(1024)S(1)} %copy-done.11, f32[512]{0:T(512)S(1)} %add_rsqrt_fusion), kind=kOutput, calls=%fused_computation.42 | convolution fusion | flops 8594128896 | bytes 27273216 | tf_op jit(solution)/shard_map/tc,ecn->ten/dot_general | solution.py:144
  126.4 4.9 %copy.40 = f32[512,8,512]{2,1,0:T(8,128)S(1)} copy(f32[512,8,512]{2,0,1:T(8,128)S(1)} %fusion.34) | data formatting | bytes 16777216 | tf_op jit(solution)/shard_map/tc,ecn->ten/dot_general | solution.py:144
  131.2 8.2 %select_reduce_fusion = f32[512,2,512]{2,1,0:T(2,128)} fusion(f32[512,8,512]{2,1,0:T(8,128)S(1)} %copy.40, pred[512,2,8]{2,1,0:T(4,128)(4,1)S(1)} %copy.38), kind=kLoop, calls=%fused_computation.25 | loop fusion | flops 7864320 | bytes 10493952 | tf_op jit(solution)/shard_map/reduce_sum | solution.py:155
  139.5 3.3 %reshape.262 = f32[1024,4,128]{2,1,0:T(4,128)S(1)} reshape(f32[512,2,512]{2,1,0:T(2,128)} %select_reduce_fusion) | data formatting | bytes 4194304 | tf_op jit(solution)/shard_map/reshape | solution.py:156
  145.8 31.3 %while.14 = (s32[]{:T(128)}, f32[4,1024]{1,0:T(4,128)S(1)}, f32[4,1024]{1,0:T(4,128)S(1)}, f32[4,1024,128]{2,1,0:T(8,128)}, s32[]{:T(128)}, /*index=5*/s32[]{:T(...) while((s32[]{:T(128)}, f32[4,1024]{1,0:T(4,128)S(1)}, ...), condition=%wide.region_7.8_spmd, body=%wide.region_4.7_spmd.sunk | while | flops 1102063616 | bytes 65276644 | solution.py:78
  146.6 2.4 bitcast_reduce_fusion.2
  149.1 2.5 fusion.78
  153.2 9.0 %multiply_add_fusion.6 = f32[4,1024,128]{2,1,0:T(8,128)} fusion(f32[4,1024,128]{2,1,0:T(8,128)} %get-tuple-element.170, f32[4,512,1024]{2,1,0:T(8,128)} %copy-done.2, f32[4,1024]{1,0:T(4,128)S(1)} %max.33, pred[512]{0:T(512)(128)(4,1)S(1)} %fusion.77, f32[4,1024]{1,0:T(4,128)S(1)} %get-tuple-element.153, ...), kind=kOutput, calls=%fused_computation.10.clone.1 | convolution fusion | flops 548405248 | bytes 13141000 | tf_op jit(solution)/shard_map/while/body/hqk,hkd->hqd/dot_general | solution.py:59
  162.9 2.4 bitcast_reduce_fusion.2
  165.3 2.5 fusion.78
  168.5 8.5 %multiply_add_fusion.6 = f32[4,1024,128]{2,1,0:T(8,128)} fusion(f32[4,1024,128]{2,1,0:T(8,128)} %get-tuple-element.170, f32[4,512,1024]{2,1,0:T(8,128)} %copy-done.2, f32[4,1024]{1,0:T(4,128)S(1)} %max.33, pred[512]{0:T(512)(128)(4,1)S(1)} %fusion.77, f32[4,1024]{1,0:T(4,128)S(1)} %get-tuple-element.153, ...), kind=kOutput, calls=%fused_computation.10.clone.1 | convolution fusion | flops 548405248 | bytes 13141000 | tf_op jit(solution)/shard_map/while/body/hqk,hkd->hqd/dot_general | solution.py:59
  177.1 5.9 %fusion.58 = f32[512,1024]{1,0:T(8,128)} fusion(bf16[2048,1024]{1,0:T(8,128)(2,1)} %all-gather.6.cloned.1.call-done, bf16[512,2048]{1,0:T(8,128)(2,1)S(1)} %copy-done.6, f32[2048]{0:T(1024)S(1)} %copy-done.11, f32[512]{0:T(512)S(1)} %add_rsqrt_fusion), kind=kOutput, calls=%fused_computation.103 | convolution fusion | flops 2151677952 | bytes 8398848 | tf_op jit(solution)/shard_map/dot_general | solution.py:143
  183.0 3.7 %reshape.263 = f32[512,4,2,128]{3,2,1,0:T(2,128)S(1)} reshape(f32[512,1024]{1,0:T(8,128)} %fusion.58) | data formatting | bytes 4194304 | tf_op jit(solution)/shard_map/reshape | solution.py:150
  191.1 2.1 fusion.22
  193.2 4.0 %divide_bitcast_fusion = f32[1024,4,128]{2,0,1:T(8,128)S(1)} fusion(f32[4,1024,128]{2,1,0:T(8,128)S(1)} %copy-done.7, f32[4,1024,512]{1,2,0:T(8,128)S(1)} %get-tuple-element.95, f32[4,1024]{1,0:T(4,128)S(1)} %max.25, pred[1024,512]{0,1:T(8,128)(4,1)S(1)} %copy-done.3, f32[4,1024]{1,0:T(4,128)S(1)} %get-tuple-element.76, ...), kind=kOutput, calls=%fused_computation.46 | convolution fusion | flops 548929536 | bytes 13680640 | tf_op jit(solution)/shard_map/hqk,hkd->hqd/dot_general | solution.py:59
  197.2 2.7 copy.45
  199.9 3.0 reshape.264
  204.8 9.1 %select_reduce_fusion.1 = bf16[512,8,512]{2,1,0:T(8,128)(2,1)} fusion(pred[512,2,8]{2,1,0:T(4,128)(4,1)S(1)} %copy.38, bf16[512,2,512]{2,1,0:T(2,128)(2,1)S(1)} %multiply_convert_fusion), kind=kLoop, calls=%fused_computation.26 | loop fusion | flops 6291456 | bytes 5251072 | tf_op jit(solution)/shard_map/reduce_sum | solution.py:184
  213.9 22.3 %all-gather.8.cloned.1.call-done = bf16[8,512,2048]{2,1,0:T(8,128)(2,1)} async-done(((bf16[8,512,256]{2,1,0:T(8,128)(2,1)}), bf16[8,512,2048]{2,1,0:T(8,128)(2,1)}) %all-gather.8.cloned.1.call-update) | async-done | bytes 16777232 | tf_op jit(solution)/shard_map/all_gather | solution.py:142
  236.2 15.3 %bitcast_convert_fusion = bf16[512,2048]{1,0:T(8,128)(2,1)S(1)} fusion(bf16[8,512,2048]{2,1,0:T(8,128)(2,1)} %all-gather.8.cloned.1.call-done, bf16[512,8,512]{2,1,0:T(8,128)(2,1)} %select_reduce_fusion.1), kind=kOutput, calls=%fused_computation.37 | convolution fusion | flops 8590983168 | bytes 23068672 | tf_op jit(solution)/shard_map/dot_general | solution.py:188
  252.6 4.2 %collective-permute-start = (bf16[128,2048]{1,0:T(8,128)(2,1)}, bf16[128,2048]{1,0:T(8,128)(2,1)}, u32[]{:S(2)}, u32[]{:S(2)}) collective-permute-start(bf16[128,2048]{1,0:T(8,128)(2,1)} %get-tuple-element.86), channel_id=1, source_target_pairs={{0,1},{4,5},{8,9},{12,13},{16,17},{20,21},{24,25},{28,29}} | collective-permute-start | bytes 1572872 | tf_op jit(solution)/shard_map/ppermute | solution.py:104
  258.2 9.6 %collective-permute-done = bf16[128,2048]{1,0:T(8,128)(2,1)} collective-permute-done((bf16[128,2048]{1,0:T(8,128)(2,1)}, bf16[128,2048]{1,0:T(8,128)(2,1)}, u32[]{:S(2)}, u32[]{:S(2)}) %collective-permute-start) | collective-permute-done | bytes 524320 | tf_op jit(solution)/shard_map/ppermute | solution.py:104
  267.9 2.6 fusion.41
  270.4 5.2 %collective-permute-start.1 = (bf16[128,2048]{1,0:T(8,128)(2,1)}, bf16[128,2048]{1,0:T(8,128)(2,1)}, u32[]{:S(2)}, u32[]{:S(2)}) collective-permute-start(bf16[128,2048]{1,0:T(8,128)(2,1)} %get-tuple-element.84), channel_id=1, source_target_pairs={{0,1},{1,2},{4,5},{5,6},{8,9},{9,10},{12,13},{13,14},{16,17},{17,1... | collective-permute-start | bytes 1572872 | tf_op jit(solution)/shard_map/ppermute | solution.py:104
  277.1 8.8 %collective-permute-done.1 = bf16[128,2048]{1,0:T(8,128)(2,1)} collective-permute-done((bf16[128,2048]{1,0:T(8,128)(2,1)}, bf16[128,2048]{1,0:T(8,128)(2,1)}, u32[]{:S(2)}, u32[]{:S(2)}) %collective-permute-start.1) | collective-permute-done | bytes 524320 | tf_op jit(solution)/shard_map/ppermute | solution.py:104
  285.9 2.6 fusion.40
  288.4 9.8 %collective-permute-start.2 = (bf16[128,2048]{1,0:T(8,128)(2,1)}, bf16[128,2048]{1,0:T(8,128)(2,1)}, u32[]{:S(2)}, u32[]{:S(2)}) collective-permute-start(bf16[128,2048]{1,0:T(8,128)(2,1)} %get-tuple-element.82), channel_id=1, source_target_pairs={{0,1},{1,2},{2,3},{4,5},{5,6},{6,7},{8,9},{9,10},{10,11},{12,13},{... | collective-permute-start | bytes 1572872 | tf_op jit(solution)/shard_map/ppermute | solution.py:104
  302.3 5.0 %collective-permute-done.2 = bf16[128,2048]{1,0:T(8,128)(2,1)} collective-permute-done((bf16[128,2048]{1,0:T(8,128)(2,1)}, bf16[128,2048]{1,0:T(8,128)(2,1)}, u32[]{:S(2)}, u32[]{:S(2)}) %collective-permute-start.2) | collective-permute-done | bytes 524320 | tf_op jit(solution)/shard_map/ppermute | solution.py:104
  307.3 4.9 %collective-permute-done.5 = bf16[128,2048]{1,0:T(8,128)(2,1)} collective-permute-done((bf16[128,2048]{1,0:T(8,128)(2,1)}, bf16[128,2048]{1,0:T(8,128)(2,1)}, u32[]{:S(2)}, u32[]{:S(2)}) %collective-permute-start.5) | collective-permute-done | bytes 524320 | tf_op jit(solution)/shard_map/ppermute | solution.py:104
  312.2 2.2 fusion.43
  (83 shorter events, 30.9 us)
Async XLA Ops:
  7.2 99.6 %copy-start = (f32[2048,8]{0,1:T(8,128)S(1)}, f32[2048,8]{0,1:T(8,128)}, u32[]{:S(2)}) copy-start(f32[2048,8]{0,1:T(8,128)} %param.13) | copy-start | bytes 196612
  7.2 96.1 %copy-start.12 = (s32[8]{0:T(128)S(1)}, s32[8]{0:T(128)}, u32[]{:S(2)}) copy-start(s32[8]{0:T(128)} %param.18) | copy-start | bytes 100
  7.2 98.6 %copy-start.10 = (s32[512,2]{0,1:T(2,128)S(1)}, s32[512,2]{0,1:T(2,128)}, u32[]{:S(2)}) copy-start(s32[512,2]{0,1:T(2,128)} %param.17) | copy-start | bytes 12292
  7.2 99.0 %copy-start.5 = (bf16[512,2048]{1,0:T(8,128)(2,1)S(1)}, bf16[512,2048]{1,0:T(8,128)(2,1)}, u32[]{:S(2)}) copy-start(bf16[512,2048]{1,0:T(8,128)(2,1)} %param.11) | copy-start | bytes 6291460
  7.2 99.5 %copy-start.11 = (f32[2048]{0:T(1024)S(1)}, f32[2048]{0:T(1024)}, u32[]{:S(2)}) copy-start(f32[2048]{0:T(1024)} %param.12) | copy-start | bytes 24580
  7.2 95.3 %all-gather.4.cloned.1.call-start = ((), (), s32[]{:S(2)}) async-start(), calls=%async_computation | async-start | bytes 18874368 | tf_op jit(solution)/shard_map/all_gather | solution.py:137
  8.0 169.1 %all-gather.6.cloned.1.call-start = ((), (), s32[]{:S(2)}) async-start(), calls=%async_computation.1 | async-start | bytes 4718592 | tf_op jit(solution)/shard_map/all_gather | solution.py:141
  102.6 133.6 %all-gather.8.cloned.1.call-start = ((), (), s32[]{:S(2)}) async-start(), calls=%async_computation.2 | async-start | bytes 18874368 | tf_op jit(solution)/shard_map/all_gather | solution.py:142
  145.8 31.3 %copy-start.6 = (bf16[512,2048]{1,0:T(8,128)(2,1)S(1)}, bf16[512,2048]{1,0:T(8,128)(2,1)}, u32[]{:S(2)}) copy-start(bf16[512,2048]{1,0:T(8,128)(2,1)} %param.11) | copy-start | bytes 6291460
  149.1 4.1 %copy-start.2 = (f32[4,512,1024]{2,1,0:T(8,128)}, f32[4,512,1024]{2,1,0:T(8,128)S(1)}, u32[]{:S(2)}) copy-start(f32[4,512,1024]{2,1,0:T(8,128)S(1)} %get-tuple-element.151) | copy-start | bytes 25165828 | tf_op jit(solution)/shard_map/while
  165.3 3.2 %copy-start.2 = (f32[4,512,1024]{2,1,0:T(8,128)}, f32[4,512,1024]{2,1,0:T(8,128)S(1)}, u32[]{:S(2)}) copy-start(f32[4,512,1024]{2,1,0:T(8,128)S(1)} %get-tuple-element.151) | copy-start | bytes 25165828 | tf_op jit(solution)/shard_map/while
  186.7 1.9 copy-start.8
  186.7 1.9 copy-start.9
  187.5 1.7 copy-start.3
  188.6 4.6 %copy-start.4 = (bf16[512,4,1,128]{3,2,1,0:T(2,128)(2,1)}, bf16[512,4,1,128]{3,2,1,0:T(2,128)(2,1)S(1)}, u32[]{:S(2)}) copy-start(bf16[512,4,1,128]{3,2,1,0:T(2,128)(2,1)S(1)} %slice.53) | copy-start | bytes 1572868
  191.0 2.2 copy-start.7
  252.6 15.3 %collective-permute-start = (bf16[128,2048]{1,0:T(8,128)(2,1)}, bf16[128,2048]{1,0:T(8,128)(2,1)}, u32[]{:S(2)}, u32[]{:S(2)}) collective-permute-start(bf16[128,2048]{1,0:T(8,128)(2,1)} %get-tuple-element.86), channel_id=1, source_target_pairs={{0,1},{4,5},{8,9},{12,13},{16,17},{20,21},{24,25},{28,29}} | collective-permute-start | bytes 1572872 | tf_op jit(solution)/shard_map/ppermute | solution.py:104
  256.7 11.1 %collective-permute-start.3 = (bf16[128,2048]{1,0:T(8,128)(2,1)}, bf16[128,2048]{1,0:T(8,128)(2,1)}, u32[]{:S(2)}, u32[]{:S(2)}) collective-permute-start(bf16[128,2048]{1,0:T(8,128)(2,1)} %get-tuple-element.87), channel_id=1, source_target_pairs={{3,2},{7,6},{11,10},{15,14},{19,18},{23,22},{27,26},{31,30}} | collective-permute-start | bytes 1572872 | tf_op jit(solution)/shard_map/ppermute | solution.py:104
  270.4 15.5 %collective-permute-start.1 = (bf16[128,2048]{1,0:T(8,128)(2,1)}, bf16[128,2048]{1,0:T(8,128)(2,1)}, u32[]{:S(2)}, u32[]{:S(2)}) collective-permute-start(bf16[128,2048]{1,0:T(8,128)(2,1)} %get-tuple-element.84), channel_id=1, source_target_pairs={{0,1},{1,2},{4,5},{5,6},{8,9},{9,10},{12,13},{13,14},{16,17},{17,1... | collective-permute-start | bytes 1572872 | tf_op jit(solution)/shard_map/ppermute | solution.py:104
  275.6 10.3 %collective-permute-start.4 = (bf16[128,2048]{1,0:T(8,128)(2,1)}, bf16[128,2048]{1,0:T(8,128)(2,1)}, u32[]{:S(2)}, u32[]{:S(2)}) collective-permute-start(bf16[128,2048]{1,0:T(8,128)(2,1)} %get-tuple-element.85), channel_id=1, source_target_pairs={{2,1},{3,2},{6,5},{7,6},{10,9},{11,10},{14,13},{15,14},{18,17},{19... | collective-permute-start | bytes 1572872 | tf_op jit(solution)/shard_map/ppermute | solution.py:104
  277.1 37.4 %copy-start.1 = (f32[2048,8]{0,1:T(8,128)S(1)}, f32[2048,8]{0,1:T(8,128)}, u32[]{:S(2)}) copy-start(f32[2048,8]{0,1:T(8,128)} %param.13) | copy-start | bytes 196612
  288.4 18.9 %collective-permute-start.2 = (bf16[128,2048]{1,0:T(8,128)(2,1)}, bf16[128,2048]{1,0:T(8,128)(2,1)}, u32[]{:S(2)}, u32[]{:S(2)}) collective-permute-start(bf16[128,2048]{1,0:T(8,128)(2,1)} %get-tuple-element.82), channel_id=1, source_target_pairs={{0,1},{1,2},{2,3},{4,5},{5,6},{6,7},{8,9},{9,10},{10,11},{12,13},{... | collective-permute-start | bytes 1572872 | tf_op jit(solution)/shard_map/ppermute | solution.py:104
  298.2 14.0 %collective-permute-start.5 = (bf16[128,2048]{1,0:T(8,128)(2,1)}, bf16[128,2048]{1,0:T(8,128)(2,1)}, u32[]{:S(2)}, u32[]{:S(2)}) collective-permute-start(bf16[128,2048]{1,0:T(8,128)(2,1)} %get-tuple-element.83), channel_id=1, source_target_pairs={{1,0},{2,1},{3,2},{5,4},{6,5},{7,6},{9,8},{10,9},{11,10},{13,12},{... | collective-permute-start | bytes 1572872 | tf_op jit(solution)/shard_map/ppermute | solution.py:104
Sparse Core Ops, SparseCore 0:
  10.0 92.5 all-gather.3
  104.4 36.7 all-gather.5
  143.1 93.1 all-gather.7
where the time goes:
time: 324 us; the launch traced here: 321 us
  waiting for transfers between devices  147 us (45%)
  matrix products  63 us (19%)
  other arithmetic  45.5 us (14%)
  local copies, waits for them, and re-layouts  27.3 us (8%)
  starting transfers between devices  23.5 us (7%)
  between operations  15 us (5%)
    all_gather x1, waiting for transfers between devices, shards(): query_full = lax.all_gather(query_weight, 'req', axis=1, tiled=True)  94.6 us
    ppermute x6, waiting for transfers between devices, run(): received = lax.ppermute(block, axis, pairs_of(step))  28.3 us
    ppermute x6, starting transfers between devices, run(): received = lax.ppermute(block, axis, pairs_of(step))  23.4 us
    all_gather x1, waiting for transfers between devices, shards(): out_full = lax.all_gather(out_weight, 'req', axis=2, tiled=True)  22.3 us
    dot_general x3, matrix products, absorb(): jnp.einsum('hqk,hkd->hqd', weights.astype(jnp.bfloat16), value_rows, pref...  21.5 us
    dot_general x1, matrix products, shards(): jnp.dot(mixture_flat, flat_piece, preferred_element_type=jnp.float32)  15.3 us
    dot_general x1, matrix products, shards(): jnp.einsum('tc,ecn->ten', normed, query_full, preferred_element_type=jnp....  11.9 us
    reduce_sum x1, other arithmetic, shards(): jnp.sum(jnp.where(one_hot[..., None], weighted[:, :, None, :], 0), axis=1)  9.1 us
  transfers between devices with their start and end apart: 9, of which 6 were waited for; matrix products, arithmetic and copies ran while one was open for 34% of the time, Pallas kernels for 0%

commit v1 on v0

--- a/solution.py
+++ b/solution.py
@@ -113,6 +113,22 @@
         lambda step: [(src, src - 1) for src in range(count - step, count) if src >= 1],
     )
     return (own + rightward + leftward).astype(parts.dtype)
+
+
+def exchange_reduce(rows, weight, axis):
+    count = lax.axis_size(axis)
+    me = lax.axis_index(axis)
+    span = rows.shape[0] // count
+    total = None
+    for shift in list(range(1, count)) + [0]:
+        target = lax.rem(me + shift, count)
+        block_rows = lax.dynamic_slice_in_dim(rows, target * span, span, 0)
+        part = jnp.dot(block_rows, weight, preferred_element_type=jnp.float32).astype(jnp.bfloat16)
+        if shift:
+            part = lax.ppermute(part, axis, [(src, (src + shift) % count) for src in range(count)])
+        part = part.astype(jnp.float32)
+        total = part if total is None else total + part
+    return total.astype(jnp.bfloat16)
 
 
 def shards(
@@ -183,10 +199,8 @@
     weighted = (gate_values[:, :, None] * heads_out).astype(jnp.bfloat16)
     mixture = jnp.sum(jnp.where(one_hot[..., None], weighted[:, :, None, :], 0), axis=1)
     mixture_flat = mixture.reshape(tok_count, experts * local_heads * head_dim)
-    weight_piece = out_full
-    flat_piece = weight_piece.reshape(experts * local_heads * head_dim, weight_piece.shape[2])
-    partial_value = jnp.dot(mixture_flat, flat_piece, preferred_element_type=jnp.float32)
-    result = chain_reduce(partial_value.astype(jnp.bfloat16), "head")
+    flat_piece = out_full.reshape(experts * local_heads * head_dim, out_full.shape[2])
+    result = exchange_reduce(mixture_flat, flat_piece, "head")
     return (result, fresh_kv[None])
 
 

time: 324 us -> 313 us (0.966)
  the two profiles are of different devices: /device:TPU:0 before, /device:TPU:11 now
where the time goes in v1:
time: 313 us; the launch traced here: 310 us
  waiting for transfers between devices  119 us (38%)
  matrix products  96.9 us (31%)
  other arithmetic  42.9 us (14%)
  local copies, waits for them, and re-layouts  32 us (10%)
  between operations  15 us (5%)
  starting transfers between devices  3.86 us (1%)
    all_gather x1, waiting for transfers between devices, shards(): query_full = lax.all_gather(query_weight, 'req', axis=1, tiled=True)  93.4 us
    dot_general x5, matrix products, absorb(): jnp.einsum('hqk,hkd->hqd', weights.astype(jnp.bfloat16), value_rows, pref...  40.2 us
    dot_general x4, matrix products, exchange_reduce(): jnp.dot(block_rows, weight, preferred_element_type=jnp.float32)  25.5 us
    ppermute x3, waiting for transfers between devices, exchange_reduce(): lax.ppermute(part, axis, [(src, (src + shift) % count) for src in range(c...  24.5 us
    reduce_sum x5, other arithmetic, absorb(): row_total = row_total * shrink + jnp.sum(weights, axis=-1)  12.2 us
    dot_general x1, matrix products, shards(): jnp.einsum('tc,ecn->ten', normed, query_full, preferred_element_type=jnp....  11.9 us
    dot_general x5, matrix products, absorb(): jnp.einsum('hqd,hkd->hqk', queries, key_rows, preferred_element_type=jnp....  11.5 us
    reduce_sum x1, other arithmetic, shards(): jnp.sum(jnp.where(one_hot[..., None], query_all[:, None], 0.0), axis=2)  8.2 us
  transfers between devices with their start and end apart: 6, of which 4 were waited for; matrix products, arithmetic and copies ran while one was open for 48% of the time, Pallas kernels for 0%

profile of v1, /device:TPU:11, one launch (start us, length us, event | category | flops | bytes accessed | tf_op | source)
XLA Modules:
  0.0 310.2 jit_solution(12866438923315046674)
XLA Ops:
  8.0 93.4 %all-gather.4.cloned.1.call-done = bf16[8,2048,512]{2,1,0:T(8,128)(2,1)} async-done(((bf16[8,256,512]{2,1,0:T(8,128)(2,1)}), bf16[8,2048,512]{2,1,0:T(8,128)(2,1)}) %all-gather.4.cloned.1.call-update) | async-done | bytes 16777232 | tf_op jit(solution)/shard_map/all_gather | solution.py:153
  108.4 2.3 multiply_cosine_fusion.1
  113.7 11.9 %fusion.31 = f32[512,8,512]{2,0,1:T(8,128)S(1)} fusion(bf16[8,2048,512]{2,1,0:T(8,128)(2,1)} %all-gather.4.cloned.1.call-done, bf16[512,2048]{1,0:T(8,128)(2,1)S(1)} %copy-done.8, f32[2048]{0:T(1024)S(1)} %copy-done.14, f32[512]{0:T(512)S(1)} %add_rsqrt_fusion), kind=kOutput, calls=%fused_computation.44 | convolution fusion | flops 8594128896 | bytes 27273216 | tf_op jit(solution)/shard_map/tc,ecn->ten/dot_general | solution.py:160
  125.6 4.9 %copy.40 = f32[512,8,512]{2,1,0:T(8,128)S(1)} copy(f32[512,8,512]{2,0,1:T(8,128)S(1)} %fusion.31) | data formatting | bytes 16777216 | tf_op jit(solution)/shard_map/tc,ecn->ten/dot_general | solution.py:160
  130.4 8.2 %select_reduce_fusion = f32[512,2,512]{2,1,0:T(2,128)} fusion(f32[512,8,512]{2,1,0:T(8,128)S(1)} %copy.40, pred[512,2,8]{2,1,0:T(4,128)(4,1)S(1)} %copy.38), kind=kLoop, calls=%fused_computation.25 | loop fusion | flops 7864320 | bytes 10493952 | tf_op jit(solution)/shard_map/reduce_sum | solution.py:171
  138.6 3.3 %reshape.253 = f32[1024,4,128]{2,1,0:T(4,128)S(1)} reshape(f32[512,2,512]{2,1,0:T(2,128)} %select_reduce_fusion) | data formatting | bytes 4194304 | tf_op jit(solution)/shard_map/reshape | solution.py:172
  144.9 62.7 %while.14 = (s32[]{:T(128)}, f32[4,1024]{1,0:T(4,128)S(1)}, f32[4,1024]{1,0:T(4,128)S(1)}, f32[4,1024,128]{2,1,0:T(8,128)}, s32[]{:T(128)}, /*index=5*/s32[]{:T(...) while((s32[]{:T(128)}, f32[4,1024]{1,0:T(4,128)S(1)}, ...), condition=%wide.region_7.8_spmd, body=%wide.region_4.7_spmd.sunk | while | flops 1102063616 | bytes 65276644 | solution.py:78
  145.8 2.4 bitcast_reduce_fusion.2
  148.2 2.5 fusion.82
  152.3 9.0 %multiply_add_fusion.6 = f32[4,1024,128]{2,1,0:T(8,128)} fusion(f32[4,1024,128]{2,1,0:T(8,128)} %get-tuple-element.164, f32[4,512,1024]{2,1,0:T(8,128)} %copy-done.2, f32[4,1024]{1,0:T(4,128)S(1)} %max.8, pred[512]{0:T(512)(128)(4,1)S(1)} %fusion.81, f32[4,1024]{1,0:T(4,128)S(1)} %get-tuple-element.147, ...), kind=kOutput, calls=%fused_computation.10.clone.1 | convolution fusion | flops 548405248 | bytes 13141000 | tf_op jit(solution)/shard_map/while/body/hqk,hkd->hqd/dot_general | solution.py:59
  162.0 2.4 bitcast_reduce_fusion.2
  164.5 2.5 fusion.82
  167.7 8.5 %multiply_add_fusion.6 = f32[4,1024,128]{2,1,0:T(8,128)} fusion(f32[4,1024,128]{2,1,0:T(8,128)} %get-tuple-element.164, f32[4,512,1024]{2,1,0:T(8,128)} %copy-done.2, f32[4,1024]{1,0:T(4,128)S(1)} %max.8, pred[512]{0:T(512)(128)(4,1)S(1)} %fusion.81, f32[4,1024]{1,0:T(4,128)S(1)} %get-tuple-element.147, ...), kind=kOutput, calls=%fused_computation.10.clone.1 | convolution fusion | flops 548405248 | bytes 13141000 | tf_op jit(solution)/shard_map/while/body/hqk,hkd->hqd/dot_general | solution.py:59
  176.9 2.4 bitcast_reduce_fusion.2
  179.3 2.5 fusion.82
  182.6 10.2 %multiply_add_fusion.6 = f32[4,1024,128]{2,1,0:T(8,128)} fusion(f32[4,1024,128]{2,1,0:T(8,128)} %get-tuple-element.164, f32[4,512,1024]{2,1,0:T(8,128)} %copy-done.2, f32[4,1024]{1,0:T(4,128)S(1)} %max.8, pred[512]{0:T(512)(128)(4,1)S(1)} %fusion.81, f32[4,1024]{1,0:T(4,128)S(1)} %get-tuple-element.147, ...), kind=kOutput, calls=%fused_computation.10.clone.1 | convolution fusion | flops 548405248 | bytes 13141000 | tf_op jit(solution)/shard_map/while/body/hqk,hkd->hqd/dot_general | solution.py:59
  193.4 2.4 bitcast_reduce_fusion.2
  195.8 2.5 fusion.82
  199.0 8.5 %multiply_add_fusion.6 = f32[4,1024,128]{2,1,0:T(8,128)} fusion(f32[4,1024,128]{2,1,0:T(8,128)} %get-tuple-element.164, f32[4,512,1024]{2,1,0:T(8,128)} %copy-done.2, f32[4,1024]{1,0:T(4,128)S(1)} %max.8, pred[512]{0:T(512)(128)(4,1)S(1)} %fusion.81, f32[4,1024]{1,0:T(4,128)S(1)} %get-tuple-element.147, ...), kind=kOutput, calls=%fused_computation.10.clone.1 | convolution fusion | flops 548405248 | bytes 13141000 | tf_op jit(solution)/shard_map/while/body/hqk,hkd->hqd/dot_general | solution.py:59
  207.6 6.0 %fusion.59 = f32[512,1024]{1,0:T(8,128)} fusion(bf16[2048,1024]{1,0:T(8,128)(2,1)} %all-gather.6.cloned.1.call-done, bf16[512,2048]{1,0:T(8,128)(2,1)S(1)} %copy-done.9, f32[2048]{0:T(1024)S(1)} %copy-done.14, f32[512]{0:T(512)S(1)} %add_rsqrt_fusion), kind=kOutput, calls=%fused_computation.101 | convolution fusion | flops 2151677952 | bytes 8398848 | tf_op jit(solution)/shard_map/dot_general | solution.py:159
  213.6 3.2 %reshape.254 = f32[512,4,2,128]{3,2,1,0:T(2,128)S(1)} reshape(f32[512,1024]{1,0:T(8,128)} %fusion.59) | data formatting | bytes 4194304 | tf_op jit(solution)/shard_map/reshape | solution.py:166
  223.4 4.0 %divide_bitcast_fusion = f32[1024,4,128]{2,0,1:T(8,128)S(1)} fusion(f32[4,1024,128]{2,1,0:T(8,128)S(1)} %copy-done.10, f32[4,1024,512]{1,2,0:T(8,128)S(1)} %get-tuple-element.89, f32[4,1024]{1,0:T(4,128)S(1)} %max.6, pred[1024,512]{0,1:T(8,128)(4,1)S(1)} %copy-done.5, f32[4,1024]{1,0:T(4,128)S(1)} %get-tuple-element.76, ...), kind=kOutput, calls=%fused_computation.48 | convolution fusion | flops 548929536 | bytes 13680640 | tf_op jit(solution)/shard_map/hqk,hkd->hqd/dot_general | solution.py:59
  227.4 2.7 copy.45
  230.0 3.3 %reshape.255 = f32[512,2,512]{2,1,0:T(2,128)S(1)} reshape(f32[1024,4,128]{2,1,0:T(4,128)} %copy.45) | data formatting | bytes 4194304 | tf_op jit(solution)/shard_map/reshape | solution.py:198
  235.3 7.2 %select_reduce_fusion.1 = bf16[512,8,512]{2,1,0:T(8,128)(2,1)S(1)} fusion(pred[512,2,8]{2,1,0:T(4,128)(4,1)S(1)} %copy.38, bf16[512,2,512]{2,1,0:T(2,128)(2,1)S(1)} %multiply_convert_fusion), kind=kLoop, calls=%fused_computation.26 | loop fusion | flops 6291456 | bytes 5251072 | tf_op jit(solution)/shard_map/reduce_sum | solution.py:200
  242.5 4.2 %copy.50 = bf16[64,8,8,512]{3,1,2,0:T(8,128)(2,1)} copy(bf16[64,8,8,512]{3,2,1,0:T(8,128)(2,1)S(1)} %bitcast.64) | data formatting | bytes 8388608
  246.7 9.4 %convolution_convert_fusion.3 = bf16[128,2048]{1,0:T(8,128)(2,1)} fusion(bf16[4096,2048]{1,0:T(8,128)(2,1)} %bitcast.59, bf16[512,4096]{1,0:T(8,128)(2,1)} %bitcast.65, s32[]{:T(128)S(6)} %select_n.72), kind=kOutput, calls=%fused_computation.43 | convolution fusion | flops 2147745792 | bytes 18350084 | tf_op jit(solution)/shard_map/dot_general | solution.py:126
  258.9 3.3 %convolution_convert_fusion.2 = bf16[128,2048]{1,0:T(8,128)(2,1)} fusion(bf16[4096,2048]{1,0:T(8,128)(2,1)S(1)} %bitcast.61, bf16[512,4096]{1,0:T(8,128)(2,1)S(1)} %bitcast.67, s32[]{:T(128)S(6)} %select_n.73), kind=kOutput, calls=%fused_computation.42 | convolution fusion | flops 2147745792 | bytes 18350084 | tf_op jit(solution)/shard_map/dot_general | solution.py:126
  264.3 3.3 %convolution_convert_fusion.1 = bf16[128,2048]{1,0:T(8,128)(2,1)} fusion(bf16[4096,2048]{1,0:T(8,128)(2,1)S(1)} %bitcast.62, bf16[512,4096]{1,0:T(8,128)(2,1)S(1)} %bitcast.68, s32[]{:T(128)S(6)} %select_n.74), kind=kOutput, calls=%fused_computation.41 | convolution fusion | flops 2147745792 | bytes 18350084 | tf_op jit(solution)/shard_map/dot_general | solution.py:126
  269.4 18.6 %collective-permute-done = bf16[128,2048]{1,0:T(8,128)(2,1)S(1)} collective-permute-done((bf16[128,2048]{1,0:T(8,128)(2,1)}, bf16[128,2048]{1,0:T(8,128)(2,1)S(1)}, u32[]{:S(2)}, u32[]{:S(2)}) %collective-permute-start) | collective-permute-done | bytes 524320 | tf_op jit(solution)/shard_map/ppermute | solution.py:128
  288.0 5.6 %collective-permute-done.1 = bf16[128,2048]{1,0:T(8,128)(2,1)} collective-permute-done((bf16[128,2048]{1,0:T(8,128)(2,1)}, bf16[128,2048]{1,0:T(8,128)(2,1)}, u32[]{:S(2)}, u32[]{:S(2)}) %collective-permute-start.1) | collective-permute-done | bytes 524320 | tf_op jit(solution)/shard_map/ppermute | solution.py:128
  294.0 9.5 %add_convert_fusion.1 = bf16[128,2048]{1,0:T(8,128)(2,1)} fusion(bf16[128,2048]{1,0:T(8,128)(2,1)} %collective-permute-done.2, bf16[128,2048]{1,0:T(8,128)(2,1)} %collective-permute-done.1, bf16[128,2048]{1,0:T(8,128)(2,1)S(1)} %collective-permute-done, bf16[4096,2048]{1,0:T(8,128)(2,1)} %bitcast.60, bf16[512,4096]{1,0:T(8,128)(2,1)} %bitcast.66, ...), kind=kOutput, calls=%fused_computation.56 | convolution fusion | flops 2149842944 | bytes 19922948 | tf_op jit(solution)/shard_map/dot_general | solution.py:126
  (101 shorter events, 34.9 us)
Async XLA Ops:
  7.2 98.4 %copy-start = (f32[2048,8]{0,1:T(8,128)S(1)}, f32[2048,8]{0,1:T(8,128)}, u32[]{:S(2)}) copy-start(f32[2048,8]{0,1:T(8,128)} %param.13) | copy-start | bytes 196612
  7.2 95.0 %copy-start.15 = (s32[8]{0:T(128)S(1)}, s32[8]{0:T(128)}, u32[]{:S(2)}) copy-start(s32[8]{0:T(128)} %param.18) | copy-start | bytes 100
  7.2 97.4 %copy-start.13 = (s32[512,2]{0,1:T(2,128)S(1)}, s32[512,2]{0,1:T(2,128)}, u32[]{:S(2)}) copy-start(s32[512,2]{0,1:T(2,128)} %param.17) | copy-start | bytes 12292
  7.2 97.9 %copy-start.8 = (bf16[512,2048]{1,0:T(8,128)(2,1)S(1)}, bf16[512,2048]{1,0:T(8,128)(2,1)}, u32[]{:S(2)}) copy-start(bf16[512,2048]{1,0:T(8,128)(2,1)} %param.11) | copy-start | bytes 6291460
  7.2 98.4 %copy-start.14 = (f32[2048]{0:T(1024)S(1)}, f32[2048]{0:T(1024)}, u32[]{:S(2)}) copy-start(f32[2048]{0:T(1024)} %param.12) | copy-start | bytes 24580
  7.2 94.2 %all-gather.4.cloned.1.call-start = ((), (), s32[]{:S(2)}) async-start(), calls=%async_computation | async-start | bytes 18874368 | tf_op jit(solution)/shard_map/all_gather | solution.py:153
  8.0 199.6 %all-gather.6.cloned.1.call-start = ((), (), s32[]{:S(2)}) async-start(), calls=%async_computation.1 | async-start | bytes 4718592 | tf_op jit(solution)/shard_map/all_gather | solution.py:157
  101.4 145.2 %all-gather.8.cloned.1.call-start = ((), (), s32[]{:S(2)}) async-start(), calls=%async_computation.2 | async-start | bytes 18874368 | tf_op jit(solution)/shard_map/all_gather | solution.py:158
  144.9 62.7 %copy-start.9 = (bf16[512,2048]{1,0:T(8,128)(2,1)S(1)}, bf16[512,2048]{1,0:T(8,128)(2,1)}, u32[]{:S(2)}) copy-start(bf16[512,2048]{1,0:T(8,128)(2,1)} %param.11) | copy-start | bytes 6291460
  148.2 4.1 %copy-start.2 = (f32[4,512,1024]{2,1,0:T(8,128)}, f32[4,512,1024]{2,1,0:T(8,128)S(1)}, u32[]{:S(2)}) copy-start(f32[4,512,1024]{2,1,0:T(8,128)S(1)} %get-tuple-element.145) | copy-start | bytes 25165828 | tf_op jit(solution)/shard_map/while
  164.4 3.2 %copy-start.2 = (f32[4,512,1024]{2,1,0:T(8,128)}, f32[4,512,1024]{2,1,0:T(8,128)S(1)}, u32[]{:S(2)}) copy-start(f32[4,512,1024]{2,1,0:T(8,128)S(1)} %get-tuple-element.145) | copy-start | bytes 25165828 | tf_op jit(solution)/shard_map/while
  179.3 3.2 %copy-start.2 = (f32[4,512,1024]{2,1,0:T(8,128)}, f32[4,512,1024]{2,1,0:T(8,128)S(1)}, u32[]{:S(2)}) copy-start(f32[4,512,1024]{2,1,0:T(8,128)S(1)} %get-tuple-element.145) | copy-start | bytes 25165828 | tf_op jit(solution)/shard_map/while
  195.8 3.2 %copy-start.2 = (f32[4,512,1024]{2,1,0:T(8,128)}, f32[4,512,1024]{2,1,0:T(8,128)S(1)}, u32[]{:S(2)}) copy-start(f32[4,512,1024]{2,1,0:T(8,128)S(1)} %get-tuple-element.145) | copy-start | bytes 25165828 | tf_op jit(solution)/shard_map/while
  216.9 1.9 copy-start.11
  216.9 1.9 copy-start.12
  217.6 1.7 copy-start.5
  218.7 4.7 %copy-start.6 = (bf16[512,4,1,128]{3,2,1,0:T(2,128)(2,1)}, bf16[512,4,1,128]{3,2,1,0:T(2,128)(2,1)S(1)}, u32[]{:S(2)}) copy-start(bf16[512,4,1,128]{3,2,1,0:T(2,128)(2,1)S(1)} %slice.53) | copy-start | bytes 1572868
  221.2 2.2 copy-start.10
  246.6 11.0 %copy-start.3 = (bf16[8,512,2048]{2,1,0:T(8,128)(2,1)S(1)}, bf16[8,512,2048]{2,1,0:T(8,128)(2,1)}, u32[]{:S(2)}) copy-start(bf16[8,512,2048]{2,1,0:T(8,128)(2,1)} %all-gather.8.cloned.1.call-done) | copy-start | bytes 50331652
  246.7 12.2 %copy-start.4 = (bf16[64,8,8,512]{3,1,2,0:T(8,128)(2,1)S(1)}, bf16[64,8,8,512]{3,1,2,0:T(8,128)(2,1)}, u32[]{:S(2)}) copy-start(bf16[64,8,8,512]{3,1,2,0:T(8,128)(2,1)} %copy.50) | copy-start | bytes 12582916
  256.0 32.0 %collective-permute-start = (bf16[128,2048]{1,0:T(8,128)(2,1)}, bf16[128,2048]{1,0:T(8,128)(2,1)S(1)}, u32[]{:S(2)}, u32[]{:S(2)}) collective-permute-start(bf16[128,2048]{1,0:T(8,128)(2,1)} %convolution_convert_fusion.3), channel_id=1, source_target_pairs={{0,1},{1,2},{2,3},{3,0},{4,5},{5,6},{6,7},{7,4},{8,9},{9,10},{10,1... | collective-permute-start | bytes 1572872 | tf_op jit(solution)/shard_map/ppermute | solution.py:128
  262.2 5.7 %copy-start.7 = (bf16[512,4,1,128]{3,2,1,0:T(2,128)(2,1)S(1)}, bf16[512,4,1,128]{3,2,1,0:T(2,128)(2,1)}, u32[]{:S(2)}) copy-start(bf16[512,4,1,128]{3,2,1,0:T(2,128)(2,1)} %copy-done.6) | copy-start | bytes 1572868
  262.2 31.4 %collective-permute-start.1 = (bf16[128,2048]{1,0:T(8,128)(2,1)}, bf16[128,2048]{1,0:T(8,128)(2,1)}, u32[]{:S(2)}, u32[]{:S(2)}) collective-permute-start(bf16[128,2048]{1,0:T(8,128)(2,1)} %convolution_convert_fusion.2), channel_id=1, source_target_pairs={{0,2},{1,3},{2,0},{3,1},{4,6},{5,7},{6,4},{7,5},{8,10},{9,11},{10,... | collective-permute-start | bytes 1572872 | tf_op jit(solution)/shard_map/ppermute | solution.py:128
  267.6 26.3 %collective-permute-start.2 = (bf16[128,2048]{1,0:T(8,128)(2,1)}, bf16[128,2048]{1,0:T(8,128)(2,1)}, u32[]{:S(2)}, u32[]{:S(2)}) collective-permute-start(bf16[128,2048]{1,0:T(8,128)(2,1)} %convolution_convert_fusion.1), channel_id=1, source_target_pairs={{0,3},{1,0},{2,1},{3,2},{4,7},{5,4},{6,5},{7,6},{8,11},{9,8},{10,9... | collective-permute-start | bytes 1572872 | tf_op jit(solution)/shard_map/ppermute | solution.py:128
  294.0 9.5 %copy-start.1 = (f32[2048,8]{0,1:T(8,128)S(1)}, f32[2048,8]{0,1:T(8,128)}, u32[]{:S(2)}) copy-start(f32[2048,8]{0,1:T(8,128)} %param.13) | copy-start | bytes 196612
Sparse Core Ops, SparseCore 0:
  10.0 91.4 all-gather.3
  103.3 36.7 all-gather.5
  141.9 93.1 all-gather.7

commit v2 on v1

--- a/solution.py
+++ b/solution.py
@@ -1,8 +1,11 @@
+import functools
 import math
 
 import jax
 import jax.numpy as jnp
 from jax import lax
+from jax.experimental import pallas as pl
+from jax.experimental.pallas import tpu as pltpu
 from jax.sharding import PartitionSpec as P
 
 NEG_LARGE = -1e30
@@ -129,6 +132,94 @@
         part = part.astype(jnp.float32)
         total = part if total is None else total + part
     return total.astype(jnp.bfloat16)
+
+
+def attention_kernel(
+    length_ref, q_ref, cache_ref, fresh_ref, out_ref, peak_ref, total_ref, accum_ref, *, cache_blocks
+):
+    q_block = pl.program_id(1)
+    kv_block = pl.program_id(2)
+    rows, head_dim = q_ref.shape[1], q_ref.shape[2]
+    span = cache_ref.shape[1]
+    length = length_ref[0]
+
+    @pl.when(kv_block == 0)
+    def _():
+        peak_ref[...] = jnp.full(peak_ref.shape, NEG_LARGE, jnp.float32)
+        total_ref[...] = jnp.zeros(total_ref.shape, jnp.float32)
+        accum_ref[...] = jnp.zeros(accum_ref.shape, jnp.float32)
+
+    def absorb_block(block, allowed):
+        queries = q_ref[0]
+        scores = lax.dot_general(
+            queries,
+            block[:, :head_dim],
+            (((1,), (1,)), ((), ())),
+            preferred_element_type=jnp.float32,
+        ) * (head_dim ** (-0.5))
+        scores = jnp.where(allowed, scores, NEG_LARGE)
+        old_peak = peak_ref[...]
+        new_peak = jnp.maximum(old_peak, jnp.max(scores, axis=-1, keepdims=True))
+        weights = jnp.where(allowed, jnp.exp(scores - new_peak), 0.0)
+        shrink = jnp.exp(old_peak - new_peak)
+        total_ref[...] = total_ref[...] * shrink + jnp.sum(weights, axis=-1, keepdims=True)
+        accum_ref[...] = accum_ref[...] * shrink + jnp.dot(
+            weights.astype(jnp.bfloat16), block[:, head_dim:], preferred_element_type=jnp.float32
+        )
+        peak_ref[...] = new_peak
+
+    @pl.when((kv_block < cache_blocks) & (kv_block * span < length))
+    def _():
+        key_index = kv_block * span + lax.broadcasted_iota(jnp.int32, (1, span), 1)
+        absorb_block(cache_ref[0], key_index < length)
+
+    @pl.when(kv_block == cache_blocks)
+    def _():
+        row_token = (q_block * rows + lax.broadcasted_iota(jnp.int32, (rows, 1), 0)) // 2
+        key_index = lax.broadcasted_iota(jnp.int32, (1, span), 1)
+        absorb_block(fresh_ref[0], key_index <= row_token)
+        out_ref[0] = accum_ref[...] / total_ref[...]
+
+
+def attend(queries, cache, fresh, length):
+    heads, query_rows, head_dim = queries.shape
+    span = fresh.shape[1]
+    cache_blocks = cache.shape[1] // span
+    rows = min(query_rows, 512)
+
+    def cache_map(h, i, j, length_ref):
+        last = jnp.maximum((length_ref[0] + span - 1) // span - 1, 0)
+        return (h, jnp.minimum(j, last), 0)
+
+    grid_spec = pltpu.PrefetchScalarGridSpec(
+        num_scalar_prefetch=1,
+        grid=(heads, query_rows // rows, cache_blocks + 1),
+        in_specs=[
+            pl.BlockSpec((1, rows, head_dim), lambda h, i, j, length_ref: (h, i, 0)),
+            pl.BlockSpec((1, span, 2 * head_dim), cache_map),
+            pl.BlockSpec((1, span, 2 * head_dim), lambda h, i, j, length_ref: (h, 0, 0)),
+        ],
+        out_specs=pl.BlockSpec((1, rows, head_dim), lambda h, i, j, length_ref: (h, i, 0)),
+        scratch_shapes=[
+            pltpu.VMEM((rows, 1), jnp.float32),
+            pltpu.VMEM((rows, 1), jnp.float32),
+            pltpu.VMEM((rows, head_dim), jnp.float32),
+        ],
+    )
+    keys_seen = 4 * heads * query_rows * (cache.shape[1] + span) * head_dim
+    return pl.pallas_call(
+        functools.partial(attention_kernel, cache_blocks=cache_blocks),
+        out_shape=jax.ShapeDtypeStruct((heads, query_rows, head_dim), jnp.float32),
+        grid_spec=grid_spec,
+        compiler_params=pltpu.CompilerParams(
+            dimension_semantics=("arbitrary", "arbitrary", "arbitrary")
+        ),
+        cost_estimate=pl.CostEstimate(
+            flops=keys_seen,
+            transcendentals=heads * query_rows * (cache.shape[1] + span),
+            bytes_accessed=2 * (cache.size + fresh.size + queries.size) + 4 * queries.size,
+        ),
+    )(jnp.reshape(length, (1,)).astype(jnp.int32), queries, cache, fresh)
 
 
 def shards(
@@ -171,30 +262,7 @@
     query_sel = jnp.sum(jnp.where(one_hot[..., None], query_all[:, None], 0.0), axis=2)
     queries = jnp.transpose(query_sel.reshape(tok_count * 2, local_heads, head_dim), (1, 0, 2))
     queries = rotate(queries, jnp.repeat(positions, 2)).astype(jnp.bfloat16)
-    own_cache = kv_cache[0]
-    query_rows = tok_count * 2
-    empty_state = (
-        jnp.full((local_heads, query_rows), NEG_LARGE, jnp.float32),
-        jnp.zeros((local_heads, query_rows), jnp.float32),
-        jnp.zeros((local_heads, query_rows, head_dim), jnp.float32),
-    )
-    carry_state = cache_pass(
-        queries,
-        own_cache,
-        0,
-        own_length,
-        0,
-        (own_length + block_len - 1) // block_len,
-        0,
-        block_len,
-        empty_state,
-    )
-    row_ids = jnp.arange(query_rows) // 2
-    causal = row_ids[:, None] >= jnp.arange(tok_count)[None, :]
-    carry_state = absorb(
-        carry_state, queries, fresh_kv[..., :head_dim], fresh_kv[..., head_dim:], causal
-    )
-    heads_out = carry_state[2] / carry_state[1][..., None]
+    heads_out = attend(queries, kv_cache[0], fresh_kv, own_length)
     heads_out = jnp.transpose(heads_out, (1, 0, 2)).reshape(tok_count, 2, local_heads * head_dim)
     weighted = (gate_values[:, :, None] * heads_out).astype(jnp.bfloat16)
     mixture = jnp.sum(jnp.where(one_hot[..., None], weighted[:, :, None, :], 0), axis=1)

time: 313 us -> 311 us (level)
  matrix products: 96.9 us -> 43 us
  waiting for transfers between devices: 119 us -> 162 us
  Pallas kernels: 0 us -> 30.6 us
  other arithmetic: 42.9 us -> 30.1 us
  local copies, waits for them, and re-layouts: 32 us -> 24.7 us
    dot_general x10 -> x0, matrix products: 51.7 us -> none  [the longest x5 40.2 us: absorb(): jnp.einsum('hqk,hkd->hqd', weights.astype(jnp.bfloat16), value_rows, pref...]
    all_gather x1, waiting for transfers between devices: 0.01 us -> 32.6 us  [shards(): out_full = lax.all_gather(out_weight, 'req', axis=2, tiled=True)]
    pallas_call x0 -> x1, Pallas kernels: none -> 30.6 us  [attend(): pl.pallas_call(functools.partial(attention_kernel, cache_blocks=cache_blo...]
    reduce_sum x5 -> x0, other arithmetic: 12.2 us -> none  [absorb(): row_total = row_total * shrink + jnp.sum(weights, axis=-1)]
    ppermute x3, waiting for transfers between devices: 24.5 us -> 34.6 us  [exchange_reduce(): lax.ppermute(part, axis, [(src, (src + shift) % count) for src in range(c...]
    while x12 -> x0, local copies, waits for them, and re-layouts: 3.62 us -> none
    reshape x1 -> x0, local copies, waits for them, and re-layouts: 3.22 us -> none  [shards(): projected = projected.reshape(tok_count, local_heads, 2, head_dim)]
    unnamed x33 -> x25, local copies, waits for them, and re-layouts: 5.93 us -> 7.04 us
  transfers between devices with their start and end apart: 6 -> 6, of which waited for: 4 -> 4; matrix products, arithmetic and copies ran while one was open for 48% -> 25% of each run, Pallas kernels for 0% -> 10%
where the time goes in v2:
time: 311 us; the launch traced here: 308 us
  waiting for transfers between devices  162 us (52%)
  matrix products  43 us (14%)
  Pallas kernels  30.6 us (10%)
  other arithmetic  30.1 us (10%)
  local copies, waits for them, and re-layouts  24.7 us (8%)
  between operations  14.2 us (5%)
  starting transfers between devices  3.91 us (1%)
    all_gather x1, waiting for transfers between devices, shards(): query_full = lax.all_gather(query_weight, 'req', axis=1, tiled=True)  93.4 us
    ppermute x3, waiting for transfers between devices, exchange_reduce(): lax.ppermute(part, axis, [(src, (src + shift) % count) for src in range(c...  34.6 us
    all_gather x1, waiting for transfers between devices, shards(): out_full = lax.all_gather(out_weight, 'req', axis=2, tiled=True)  32.6 us
    pallas_call x1, Pallas kernels, attend(): pl.pallas_call(functools.partial(attention_kernel, cache_blocks=cache_blo...  30.6 us
    dot_general x4, matrix products, exchange_reduce(): jnp.dot(block_rows, weight, preferred_element_type=jnp.float32)  24.6 us
    dot_general x1, matrix products, shards(): jnp.einsum('tc,ecn->ten', normed, query_full, preferred_element_type=jnp....  12 us
    reduce_sum x1, other arithmetic, shards(): jnp.sum(jnp.where(one_hot[..., None], query_all[:, None], 0.0), axis=2)  8.02 us
    reduce_sum x1, other arithmetic, shards(): jnp.sum(jnp.where(one_hot[..., None], weighted[:, :, None, :], 0), axis=1)  7.15 us
  transfers between devices with their start and end apart: 6, of which 4 were waited for; matrix products, arithmetic and copies ran while one was open for 25% of the time, Pallas kernels for 10%

profile of v2, /device:TPU:11, one launch (start us, length us, event | category | flops | bytes accessed | tf_op | source)
XLA Modules:
  0.0 308.4 jit_solution(3348422836778058635)
XLA Ops:
  8.0 93.4 %all-gather.4.cloned.1.call-done = bf16[8,2048,512]{2,1,0:T(8,128)(2,1)} async-done(((bf16[8,256,512]{2,1,0:T(8,128)(2,1)}), bf16[8,2048,512]{2,1,0:T(8,128)(2,1)}) %all-gather.4.cloned.1.call-update) | async-done | bytes 16777232 | tf_op jit(solution)/shard_map/all_gather | solution.py:244
  104.8 1.8 fusion.20
  106.7 0.9 copy.32
  107.6 2.0 multiply_cosine_fusion.1
  109.5 1.9 multiply_cosine_fusion
  111.4 12.0 %fusion.4 = f32[512,8,512]{2,0,1:T(8,128)S(1)} fusion(bf16[8,2048,512]{2,1,0:T(8,128)(2,1)} %all-gather.4.cloned.1.call-done, bf16[512,2048]{1,0:T(8,128)(2,1)S(1)} %copy-done.6, f32[2048]{0:T(1024)S(1)} %copy-done.9, f32[512]{0:T(512)S(1)} %add_rsqrt_fusion), kind=kOutput, calls=%fused_computation.12 | convolution fusion | flops 8594128896 | bytes 27273216 | tf_op jit(solution)/shard_map/tc,ecn->ten/dot_general | solution.py:251
  123.4 4.9 %copy.33 = f32[512,8,512]{2,1,0:T(8,128)S(1)} copy(f32[512,8,512]{2,0,1:T(8,128)S(1)} %fusion.4) | data formatting | bytes 16777216 | tf_op jit(solution)/shard_map/tc,ecn->ten/dot_general | solution.py:251
  128.3 8.0 %select_reduce_fusion = f32[512,2,512]{2,1,0:T(2,128)} fusion(f32[512,8,512]{2,1,0:T(8,128)S(1)} %copy.33, pred[512,2,8]{2,1,0:T(4,128)(4,1)S(1)} %copy.31), kind=kLoop, calls=%fused_computation | loop fusion | flops 7864320 | bytes 10493952 | tf_op jit(solution)/shard_map/reduce_sum | solution.py:262
  136.3 3.5 %reshape.213 = f32[1024,4,128]{2,1,0:T(4,128)S(1)} reshape(f32[512,2,512]{2,1,0:T(2,128)} %select_reduce_fusion) | data formatting | bytes 4194304 | tf_op jit(solution)/shard_map/reshape | solution.py:263
  139.9 0.7 subtract_convert_fusion
  140.7 1.5 pad_maximum_fusion.q_ref
  142.2 4.7 %fusion.17 = f32[512,1024]{0,1:T(8,128)S(1)} fusion(bf16[2048,1024]{1,0:T(8,128)(2,1)} %all-gather.6.cloned.1.call-done, bf16[512,2048]{1,0:T(8,128)(2,1)S(1)} %copy-done.7, f32[2048]{0:T(1024)S(1)} %copy-done.9, f32[512]{0:T(512)S(1)} %add_rsqrt_fusion), kind=kOutput, calls=%fused_computation.49 | convolution fusion | flops 2151677952 | bytes 8398848 | tf_op jit(solution)/shard_map/dot_general | solution.py:250
  147.7 1.7 subtract_convert_fusion.1
  149.4 1.4 pad_maximum_fusion.1.fresh_ref
  150.8 30.6 %shard_map.104 = f32[4,1024,128]{2,1,0:T(8,128)} custom-call(s32[1]{0:T(128)} %bitcast.length_ref, bf16[4,1024,128]{2,1,0:T(8,128)(2,1)} %pad_maximum_fusion.q_ref, bf16[4,2048,256]{2,1,0:T(8,128)(2,1)} %bitcast.52, bf16[4,512,256]{2,1,0:T(8,128)(2,1)} %pad_maximum_fusion.1.fresh_ref), custom_call_target="tpu_custom_call" | custom-call | flops 5368709120 | bytes 8388608 | tf_op jit(solution)/shard_map/pallas_call | solution.py:210
  181.4 4.6 %copy.38 = f32[1024,4,128]{2,1,0:T(4,128)} copy(f32[1024,4,128]{2,0,1:T(8,128)} %bitcast.49) | data formatting | bytes 4194304 | tf_op jit(solution)/shard_map/transpose | solution.py:266
  186.0 2.9 reshape.215
  188.9 2.3 multiply_convert_fusion
  191.2 7.2 %select_reduce_fusion.1 = bf16[512,8,512]{2,1,0:T(8,128)(2,1)S(1)} fusion(pred[512,2,8]{2,1,0:T(4,128)(4,1)S(1)} %copy.31, bf16[512,2,512]{2,1,0:T(2,128)(2,1)S(1)} %multiply_convert_fusion), kind=kLoop, calls=%fused_computation.1 | loop fusion | flops 6291456 | bytes 5251072 | tf_op jit(solution)/shard_map/reduce_sum | solution.py:268
  198.3 4.2 %copy.42 = bf16[64,8,8,512]{3,1,2,0:T(8,128)(2,1)} copy(bf16[64,8,8,512]{3,2,1,0:T(8,128)(2,1)S(1)} %bitcast.39) | data formatting | bytes 8388608
  202.5 32.6 %all-gather.8.cloned.1.call-done = bf16[8,512,2048]{2,1,0:T(8,128)(2,1)} async-done(((bf16[8,512,256]{2,1,0:T(8,128)(2,1)}), bf16[8,512,2048]{2,1,0:T(8,128)(2,1)}) %all-gather.8.cloned.1.call-update) | async-done | bytes 16777232 | tf_op jit(solution)/shard_map/all_gather | solution.py:249
  235.1 8.6 %convolution_convert_fusion.3 = bf16[128,2048]{1,0:T(8,128)(2,1)S(1)} fusion(bf16[4096,2048]{1,0:T(8,128)(2,1)} %bitcast.34, bf16[512,4096]{1,0:T(8,128)(2,1)} %bitcast.40, s32[]{:T(128)S(6)} %select_n.32), kind=kOutput, calls=%fused_computation.11 | convolution fusion | flops 2147745792 | bytes 18350084 | tf_op jit(solution)/shard_map/dot_general | solution.py:129
  243.7 1.3 collective-permute-start
  244.9 1.0 copy-done.2
  246.0 1.2 copy-done.3
  247.1 3.3 %convolution_convert_fusion.2 = bf16[128,2048]{1,0:T(8,128)(2,1)} fusion(bf16[4096,2048]{1,0:T(8,128)(2,1)S(1)} %bitcast.36, bf16[512,4096]{1,0:T(8,128)(2,1)S(1)} %bitcast.42, s32[]{:T(128)S(6)} %select_n.33), kind=kOutput, calls=%fused_computation.10 | convolution fusion | flops 2147745792 | bytes 18350084 | tf_op jit(solution)/shard_map/dot_general | solution.py:129
  250.5 2.1 collective-permute-start.1
  252.6 3.3 %convolution_convert_fusion.1 = bf16[128,2048]{1,0:T(8,128)(2,1)} fusion(bf16[4096,2048]{1,0:T(8,128)(2,1)S(1)} %bitcast.37, bf16[512,4096]{1,0:T(8,128)(2,1)S(1)} %bitcast.43, s32[]{:T(128)S(6)} %select_n.34), kind=kOutput, calls=%fused_computation.9 | convolution fusion | flops 2147745792 | bytes 18350084 | tf_op jit(solution)/shard_map/dot_general | solution.py:129
  256.3 1.4 pad_maximum_fusion.2
  257.7 32.1 %collective-permute-done.1 = bf16[128,2048]{1,0:T(8,128)(2,1)S(1)} collective-permute-done((bf16[128,2048]{1,0:T(8,128)(2,1)}, bf16[128,2048]{1,0:T(8,128)(2,1)S(1)}, u32[]{:S(2)}, u32[]{:S(2)}) %collective-permute-start.1) | collective-permute-done | bytes 524320 | tf_op jit(solution)/shard_map/ppermute | solution.py:131
  289.8 2.5 collective-permute-done.2
  292.3 9.4 %add_convert_fusion.1 = bf16[128,2048]{1,0:T(8,128)(2,1)} fusion(bf16[128,2048]{1,0:T(8,128)(2,1)} %collective-permute-done.2, bf16[128,2048]{1,0:T(8,128)(2,1)S(1)} %collective-permute-done.1, bf16[128,2048]{1,0:T(8,128)(2,1)S(1)} %collective-permute-done, bf16[4096,2048]{1,0:T(8,128)(2,1)} %bitcast.35, bf16[512,4096]{1,0:T(8,128)(2,1)} %bitcast.41, ...), kind=kOutput, calls=%fused_computation.21 | convolution fusion | flops 2149842944 | bytes 19922948 | tf_op jit(solution)/shard_map/dot_general | solution.py:129
  (47 shorter events, 5.4 us)
Async XLA Ops:
  7.2 97.6 %copy-start = (f32[2048,8]{0,1:T(8,128)S(1)}, f32[2048,8]{0,1:T(8,128)}, u32[]{:S(2)}) copy-start(f32[2048,8]{0,1:T(8,128)} %param.11) | copy-start | bytes 196612
  7.2 95.0 %copy-start.8 = (s32[512,2]{0,1:T(2,128)S(1)}, s32[512,2]{0,1:T(2,128)}, u32[]{:S(2)}) copy-start(s32[512,2]{0,1:T(2,128)} %param.15) | copy-start | bytes 12292
  7.2 95.5 %copy-start.10 = (s32[8]{0:T(128)S(1)}, s32[8]{0:T(128)}, u32[]{:S(2)}) copy-start(s32[8]{0:T(128)} %param.16) | copy-start | bytes 100
  7.2 97.1 %copy-start.6 = (bf16[512,2048]{1,0:T(8,128)(2,1)S(1)}, bf16[512,2048]{1,0:T(8,128)(2,1)}, u32[]{:S(2)}) copy-start(bf16[512,2048]{1,0:T(8,128)(2,1)} %param.9) | copy-start | bytes 6291460
  7.2 97.6 %copy-start.9 = (f32[2048]{0:T(1024)S(1)}, f32[2048]{0:T(1024)}, u32[]{:S(2)}) copy-start(f32[2048]{0:T(1024)} %param.10) | copy-start | bytes 24580
  7.2 94.2 %all-gather.4.cloned.1.call-start = ((), (), s32[]{:S(2)}) async-start(), calls=%async_computation | async-start | bytes 18874368 | tf_op jit(solution)/shard_map/all_gather | solution.py:244
  8.0 134.3 %all-gather.6.cloned.1.call-start = ((), (), s32[]{:S(2)}) async-start(), calls=%async_computation.1 | async-start | bytes 4718592 | tf_op jit(solution)/shard_map/all_gather | solution.py:248
  101.4 133.7 %all-gather.8.cloned.1.call-start = ((), (), s32[]{:S(2)}) async-start(), calls=%async_computation.2 | async-start | bytes 18874368 | tf_op jit(solution)/shard_map/all_gather | solution.py:249
  139.9 2.3 copy-start.7
  147.7 33.7 %copy-start.4 = (bf16[512,4,1,128]{3,0,1,2:T(8,128)(2,1)}, bf16[512,4,1,128]{3,0,1,2:T(8,128)(2,1)S(1)}, u32[]{:S(2)}) copy-start(bf16[512,4,1,128]{3,0,1,2:T(8,128)(2,1)S(1)} %copy.41) | copy-start | bytes 1572868
  235.1 10.9 %copy-start.2 = (bf16[8,512,2048]{2,1,0:T(8,128)(2,1)S(1)}, bf16[8,512,2048]{2,1,0:T(8,128)(2,1)}, u32[]{:S(2)}) copy-start(bf16[8,512,2048]{2,1,0:T(8,128)(2,1)} %all-gather.8.cloned.1.call-done) | copy-start | bytes 50331652
  235.1 12.0 %copy-start.3 = (bf16[64,8,8,512]{3,1,2,0:T(8,128)(2,1)S(1)}, bf16[64,8,8,512]{3,1,2,0:T(8,128)(2,1)}, u32[]{:S(2)}) copy-start(bf16[64,8,8,512]{3,1,2,0:T(8,128)(2,1)} %copy.42) | copy-start | bytes 12582916
  243.7 14.1 %collective-permute-start = (bf16[128,2048]{1,0:T(8,128)(2,1)S(1)}, bf16[128,2048]{1,0:T(8,128)(2,1)S(1)}, u32[]{:S(2)}, u32[]{:S(2)}) collective-permute-start(bf16[128,2048]{1,0:T(8,128)(2,1)S(1)} %convolution_convert_fusion.3), channel_id=1, source_target_pairs={{0,1},{1,2},{2,3},{3,0},{4,5},{5,6},{6,7},{7,4},{8,9},{9,10},{10,1... | collective-permute-start | bytes 1572872 | tf_op jit(solution)/shard_map/ppermute | solution.py:131
  250.5 5.8 %copy-start.5 = (bf16[512,4,1,128]{3,0,1,2:T(8,128)(2,1)S(1)}, bf16[512,4,1,128]{3,0,1,2:T(8,128)(2,1)}, u32[]{:S(2)}) copy-start(bf16[512,4,1,128]{3,0,1,2:T(8,128)(2,1)} %copy-done.4) | copy-start | bytes 1572868
  250.5 39.3 %collective-permute-start.1 = (bf16[128,2048]{1,0:T(8,128)(2,1)}, bf16[128,2048]{1,0:T(8,128)(2,1)S(1)}, u32[]{:S(2)}, u32[]{:S(2)}) collective-permute-start(bf16[128,2048]{1,0:T(8,128)(2,1)} %convolution_convert_fusion.2), channel_id=1, source_target_pairs={{0,2},{1,3},{2,0},{3,1},{4,6},{5,7},{6,4},{7,5},{8,10},{9,11},{10,... | collective-permute-start | bytes 1572872 | tf_op jit(solution)/shard_map/ppermute | solution.py:131
  255.9 36.4 %collective-permute-start.2 = (bf16[128,2048]{1,0:T(8,128)(2,1)}, bf16[128,2048]{1,0:T(8,128)(2,1)}, u32[]{:S(2)}, u32[]{:S(2)}) collective-permute-start(bf16[128,2048]{1,0:T(8,128)(2,1)} %convolution_convert_fusion.1), channel_id=1, source_target_pairs={{0,3},{1,0},{2,1},{3,2},{4,7},{5,4},{6,5},{7,6},{8,11},{9,8},{10,9... | collective-permute-start | bytes 1572872 | tf_op jit(solution)/shard_map/ppermute | solution.py:131
  292.3 9.4 %copy-start.1 = (f32[2048,8]{0,1:T(8,128)S(1)}, f32[2048,8]{0,1:T(8,128)}, u32[]{:S(2)}) copy-start(f32[2048,8]{0,1:T(8,128)} %param.11) | copy-start | bytes 196612
Sparse Core Ops, SparseCore 0:
  10.0 91.4 all-gather.3
  103.3 36.7 all-gather.5
  142.0 93.0 all-gather.7

commit v3 on v2

--- a/solution.py
+++ b/solution.py
@@ -139,7 +139,7 @@
 ):
     q_block = pl.program_id(1)
     kv_block = pl.program_id(2)
-    rows, head_dim = q_ref.shape[1], q_ref.shape[2]
+    rows, head_dim = q_ref.shape
     span = cache_ref.shape[1]
     length = length_ref[0]
 
@@ -150,7 +150,7 @@
         accum_ref[...] = jnp.zeros(accum_ref.shape, jnp.float32)
 
     def absorb_block(block, allowed):
-        queries = q_ref[0]
+        queries = q_ref[...]
         scores = lax.dot_general(
             queries,
             block[:, :head_dim],
@@ -175,15 +175,15 @@
 
     @pl.when(kv_block == cache_blocks)
     def _():
-        row_token = (q_block * rows + lax.broadcasted_iota(jnp.int32, (rows, 1), 0)) // 2
+        row_token = (q_block * rows + lax.broadcasted_iota(jnp.int32, (rows, 1), 0)) % span
         key_index = lax.broadcasted_iota(jnp.int32, (1, span), 1)
         absorb_block(fresh_ref[0], key_index <= row_token)
-        out_ref[0] = accum_ref[...] / total_ref[...]
+        out_ref[...] = accum_ref[...] / total_ref[...]
 
 
 def attend(queries, cache, fresh, length):
-    heads, query_rows, head_dim = queries.shape
-    span = fresh.shape[1]
+    heads, span, head_dim = fresh.shape[0], fresh.shape[1], fresh.shape[2] // 2
+    query_rows = queries.shape[0]
     cache_blocks = cache.shape[1] // span
     rows = min(query_rows, 512)
 
@@ -195,11 +195,11 @@
         num_scalar_prefetch=1,
         grid=(heads, query_rows // rows, cache_blocks + 1),
         in_specs=[
-            pl.BlockSpec((1, rows, head_dim), lambda h, i, j, length_ref: (h, i, 0)),
+            pl.BlockSpec((rows, head_dim), lambda h, i, j, length_ref: (i, h)),
             pl.BlockSpec((1, span, 2 * head_dim), cache_map),
             pl.BlockSpec((1, span, 2 * head_dim), lambda h, i, j, length_ref: (h, 0, 0)),
         ],
-        out_specs=pl.BlockSpec((1, rows, head_dim), lambda h, i, j, length_ref: (h, i, 0)),
+        out_specs=pl.BlockSpec((rows, head_dim), lambda h, i, j, length_ref: (i, h)),
         scratch_shapes=[
             pltpu.VMEM((rows, 1), jnp.float32),
             pltpu.VMEM((rows, 1), jnp.float32),
@@ -209,7 +209,7 @@
     keys_seen = 4 * heads * query_rows * (cache.shape[1] + span) * head_dim
     return pl.pallas_call(
         functools.partial(attention_kernel, cache_blocks=cache_blocks),
-        out_shape=jax.ShapeDtypeStruct((heads, query_rows, head_dim), jnp.float32),
+        out_shape=jax.ShapeDtypeStruct(queries.shape, jnp.float32),
         grid_spec=grid_spec,
         compiler_params=pltpu.CompilerParams(
             dimension_semantics=("arbitrary", "arbitrary", "arbitrary")
@@ -249,7 +249,7 @@
     out_full = lax.all_gather(out_weight, "req", axis=2, tiled=True)
     projected = jnp.dot(normed, kv_full, preferred_element_type=jnp.float32)
     query_all = jnp.einsum(
-        "tc,ecn->ten", normed, query_full, preferred_element_type=jnp.float32
+        "tc,ecn->etn", normed, query_full, preferred_element_type=jnp.float32
     )
     req_index = lax.axis_index("req")
     own_length = pick_length(lengths, req_index)
@@ -259,13 +259,16 @@
     new_values = jnp.transpose(projected[:, :, 1], (1, 0, 2))
     fresh_kv = jnp.concatenate([new_keys, new_values], axis=-1).astype(jnp.bfloat16)
     one_hot = jnp.arange(experts)[None, None, :] == expert_ids[:, :, None]
-    query_sel = jnp.sum(jnp.where(one_hot[..., None], query_all[:, None], 0.0), axis=2)
-    queries = jnp.transpose(query_sel.reshape(tok_count * 2, local_heads, head_dim), (1, 0, 2))
-    queries = rotate(queries, jnp.repeat(positions, 2)).astype(jnp.bfloat16)
+    choice_hot = jnp.transpose(one_hot, (1, 2, 0))
+    query_sel = jnp.sum(jnp.where(choice_hot[..., None], query_all[None], 0.0), axis=1)
+    query_sel = query_sel.reshape(2, tok_count, local_heads, head_dim)
+    queries = rotate(query_sel, positions[:, None]).astype(jnp.bfloat16)
+    queries = queries.reshape(2 * tok_count, local_heads * head_dim)
     heads_out = attend(queries, kv_cache[0], fresh_kv, own_length)
-    heads_out = jnp.transpose(heads_out, (1, 0, 2)).reshape(tok_count, 2, local_heads * head_dim)
-    weighted = (gate_values[:, :, None] * heads_out).astype(jnp.bfloat16)
-    mixture = jnp.sum(jnp.where(one_hot[..., None], weighted[:, :, None, :], 0), axis=1)
+    heads_out = heads_out.reshape(2, tok_count, local_heads * head_dim)
+    weighted = (jnp.transpose(gate_values)[:, :, None] * heads_out).astype(jnp.bfloat16)
+    token_hot = jnp.transpose(one_hot, (1, 0, 2))
+    mixture = jnp.sum(jnp.where(token_hot[..., None], weighted[:, :, None, :], 0), axis=0)
     mixture_flat = mixture.reshape(tok_count, experts * local_heads * head_dim)
     flat_piece = out_full.reshape(experts * local_heads * head_dim, out_full.shape[2])
     result = exchange_reduce(mixture_flat, flat_piece, "head")

time: 311 us -> 309 us (level)
  Pallas kernels: 30.6 us -> 40.4 us
  waiting for transfers between devices: 162 us -> 157 us
  other arithmetic: 30.1 us -> 26.2 us
  local copies, waits for them, and re-layouts: 24.7 us -> 21.5 us
    pallas_call x1, Pallas kernels: 30.6 us -> 40.4 us  [attend(): pl.pallas_call(functools.partial(attention_kernel, cache_blocks=cache_blo...]
    all_gather x1, waiting for transfers between devices: 32.6 us -> 27.1 us  [shards(): out_full = lax.all_gather(out_weight, 'req', axis=2, tiled=True)]
    dot_general x1 -> x0, local copies, waits for them, and re-layouts: 4.86 us -> none  [shards(): jnp.einsum('tc,ecn->ten', normed, query_full, preferred_element_type=jnp....]
    transpose x1, local copies, waits for them, and re-layouts: 4.6 us -> 9.27 us  [shards(): jnp.einsum('tc,ecn->etn', normed, query_full, preferred_element_type=jnp....]
    reshape x3 -> x1, local copies, waits for them, and re-layouts: 6.48 us -> 1.93 us  [shards(): query_sel = query_sel.reshape(2, tok_count, local_heads, head_dim)]
    unnamed x25 -> x22, local copies, waits for them, and re-layouts: 7.04 us -> 9.34 us
  transfers between devices with their start and end apart: 6 -> 6, of which waited for: 4 -> 4; matrix products, arithmetic and copies ran while one was open for 25% -> 24% of each run, Pallas kernels for 10% -> 13%
where the time goes in v3:
time: 309 us; the launch traced here: 308 us
  waiting for transfers between devices  157 us (51%)
  matrix products  45.7 us (15%)
  Pallas kernels  40.4 us (13%)
  other arithmetic  26.2 us (8%)
  local copies, waits for them, and re-layouts  21.5 us (7%)
  between operations  14 us (5%)
  starting transfers between devices  3.76 us (1%)
    all_gather x1, waiting for transfers between devices, shards(): query_full = lax.all_gather(query_weight, 'req', axis=1, tiled=True)  93.4 us
    pallas_call x1, Pallas kernels, attend(): pl.pallas_call(functools.partial(attention_kernel, cache_blocks=cache_blo...  40.4 us
    ppermute x3, waiting for transfers between devices, exchange_reduce(): lax.ppermute(part, axis, [(src, (src + shift) % count) for src in range(c...  34.8 us
    all_gather x1, waiting for transfers between devices, shards(): out_full = lax.all_gather(out_weight, 'req', axis=2, tiled=True)  27.1 us
    dot_general x4, matrix products, exchange_reduce(): jnp.dot(block_rows, weight, preferred_element_type=jnp.float32)  24.5 us
    dot_general x1, matrix products, shards(): jnp.einsum('tc,ecn->etn', normed, query_full, preferred_element_type=jnp....  14.8 us
    unnamed x22, local copies, waits for them, and re-layouts  9.34 us
    transpose x1, local copies, waits for them, and re-layouts, shards(): jnp.einsum('tc,ecn->etn', normed, query_full, preferred_element_type=jnp....  9.27 us
  transfers between devices with their start and end apart: 6, of which 4 were waited for; matrix products, arithmetic and copies ran while one was open for 24% of the time, Pallas kernels for 13%

profile of v3, /device:TPU:11, one launch (start us, length us, event | category | flops | bytes accessed | tf_op | source)
XLA Modules:
  0.0 308.2 jit_solution(6839118972061355941)
XLA Ops:
  7.3 0.7 all-gather.4.cloned.1.call-update
  8.0 93.4 %all-gather.4.cloned.1.call-done = bf16[8,2048,512]{2,1,0:T(8,128)(2,1)} async-done(((bf16[8,256,512]{2,1,0:T(8,128)(2,1)}), bf16[8,2048,512]{2,1,0:T(8,128)(2,1)}) %all-gather.4.cloned.1.call-update) | async-done | bytes 16777232 | tf_op jit(solution)/shard_map/all_gather | solution.py:244
  101.5 0.7 all-gather.8.cloned.1.call-update
  104.0 1.8 fusion.19
  106.1 1.0 multiply_cosine_fusion
  107.1 14.8 %convolution_bitcast_fusion = f32[8,512,512]{1,2,0:T(8,128)} fusion(bf16[8,2048,512]{2,1,0:T(8,128)(2,1)} %all-gather.4.cloned.1.call-done, bf16[512,2048]{1,0:T(8,128)(2,1)S(1)} %copy-done.4, f32[2048]{0:T(1024)S(1)} %copy-done.7, f32[512]{0:T(512)S(1)} %add_rsqrt_fusion), kind=kOutput, calls=%fused_computation.7 | convolution fusion | flops 8594128896 | bytes 27273216 | tf_op jit(solution)/shard_map/tc,ecn->etn/dot_general | solution.py:251
  121.9 9.3 %copy.23 = f32[8,512,512]{2,1,0:T(8,128)} copy(f32[8,512,512]{1,2,0:T(8,128)} %convolution_bitcast_fusion) | data formatting | bytes 16777216 | tf_op jit(solution)/shard_map/tc,ecn->etn/transpose | solution.py:251
  131.1 6.3 %select_reduce_fusion = f32[2,512,512]{2,1,0:T(8,128)} fusion(f32[8,512,512]{2,1,0:T(8,128)} %copy.23, pred[2,8,512]{2,1,0:T(8,128)(4,1)S(1)} %iota_compare_fusion.1), kind=kLoop, calls=%fused_computation | loop fusion | flops 7864320 | bytes 10493952 | tf_op jit(solution)/shard_map/reduce_sum | solution.py:263
  137.4 1.9 reshape.242
  139.4 1.7 subtract_convert_fusion
  141.1 1.4 pad_maximum_fusion
  142.5 1.2 copy.34
  143.7 4.6 %fusion.16 = f32[512,1024]{0,1:T(8,128)S(1)} fusion(bf16[2048,1024]{1,0:T(8,128)(2,1)} %all-gather.6.cloned.1.call-done, bf16[512,2048]{1,0:T(8,128)(2,1)S(1)} %copy-done.5, f32[2048]{0:T(1024)S(1)} %copy-done.7, f32[512]{0:T(512)S(1)} %add_rsqrt_fusion), kind=kOutput, calls=%fused_computation.49 | convolution fusion | flops 2151677952 | bytes 8398848 | tf_op jit(solution)/shard_map/dot_general | solution.py:250
  148.4 0.9 slice.39
  149.6 1.4 copy.30
  151.5 1.4 pad_maximum_fusion.1.fresh_ref
  152.9 40.4 %shard_map.104 = f32[1024,512]{1,0:T(8,128)} custom-call(s32[1]{0:T(128)} %bitcast.2.length_ref, bf16[1024,512]{1,0:T(8,128)(2,1)} %bitcast.59, bf16[4,2048,256]{2,1,0:T(8,128)(2,1)} %bitcast.62, bf16[4,512,256]{2,1,0:T(8,128)(2,1)} %pad_maximum_fusion.1.fresh_ref), custom_call_target="tpu_custom_call" | custom-call | flops 5368709120 | bytes 8388608 | tf_op jit(solution)/shard_map/pallas_call | solution.py:210
  193.4 1.8 multiply_convert_fusion
  195.2 8.6 %select_reduce_fusion.1 = bf16[512,8,512]{2,1,0:T(8,128)(2,1)S(1)} fusion(pred[2,512,8]{2,1,0:T(8,128)(4,1)S(1)} %iota_compare_fusion, bf16[2,512,512]{2,1,0:T(8,128)(2,1)S(1)} %multiply_convert_fusion), kind=kLoop, calls=%fused_computation.1 | loop fusion | flops 6291456 | bytes 5251072 | tf_op jit(solution)/shard_map/reduce_sum | solution.py:271
  203.8 4.2 %copy.32 = bf16[64,8,8,512]{3,1,2,0:T(8,128)(2,1)} copy(bf16[64,8,8,512]{3,2,1,0:T(8,128)(2,1)S(1)} %bitcast.45) | data formatting | bytes 8388608
  208.0 27.1 %all-gather.8.cloned.1.call-done = bf16[8,512,2048]{2,1,0:T(8,128)(2,1)} async-done(((bf16[8,512,256]{2,1,0:T(8,128)(2,1)}), bf16[8,512,2048]{2,1,0:T(8,128)(2,1)}) %all-gather.8.cloned.1.call-update) | async-done | bytes 16777232 | tf_op jit(solution)/shard_map/all_gather | solution.py:249
  235.1 8.6 %convolution_convert_fusion.3 = bf16[128,2048]{1,0:T(8,128)(2,1)S(1)} fusion(bf16[4096,2048]{1,0:T(8,128)(2,1)} %bitcast.41, bf16[512,4096]{1,0:T(8,128)(2,1)} %bitcast.46, s32[]{:T(128)S(6)} %select_n.32), kind=kOutput, calls=%fused_computation.12 | convolution fusion | flops 2147745792 | bytes 18350084 | tf_op jit(solution)/shard_map/dot_general | solution.py:129
  243.7 1.3 collective-permute-start
  244.9 1.0 copy-done.2
  245.9 1.2 copy-done.3
  247.1 3.3 %convolution_convert_fusion.2 = bf16[128,2048]{1,0:T(8,128)(2,1)} fusion(bf16[4096,2048]{1,0:T(8,128)(2,1)S(1)} %bitcast.43, bf16[512,4096]{1,0:T(8,128)(2,1)S(1)} %bitcast.48, s32[]{:T(128)S(6)} %select_n.33), kind=kOutput, calls=%fused_computation.11 | convolution fusion | flops 2147745792 | bytes 18350084 | tf_op jit(solution)/shard_map/dot_general | solution.py:129
  250.4 2.1 collective-permute-start.1
  252.5 3.3 %convolution_convert_fusion.1 = bf16[128,2048]{1,0:T(8,128)(2,1)} fusion(bf16[4096,2048]{1,0:T(8,128)(2,1)S(1)} %bitcast.44, bf16[512,4096]{1,0:T(8,128)(2,1)S(1)} %bitcast.49, s32[]{:T(128)S(6)} %select_n.34), kind=kOutput, calls=%fused_computation.10 | convolution fusion | flops 2147745792 | bytes 18350084 | tf_op jit(solution)/shard_map/dot_general | solution.py:129
  256.1 1.4 pad_maximum_fusion.2
  257.5 32.3 %collective-permute-done.1 = bf16[128,2048]{1,0:T(8,128)(2,1)S(1)} collective-permute-done((bf16[128,2048]{1,0:T(8,128)(2,1)}, bf16[128,2048]{1,0:T(8,128)(2,1)S(1)}, u32[]{:S(2)}, u32[]{:S(2)}) %collective-permute-start.1) | collective-permute-done | bytes 524320 | tf_op jit(solution)/shard_map/ppermute | solution.py:131
  289.8 2.5 collective-permute-done.2
  292.3 9.4 %add_convert_fusion.1 = bf16[128,2048]{1,0:T(8,128)(2,1)} fusion(bf16[128,2048]{1,0:T(8,128)(2,1)} %collective-permute-done.2, bf16[128,2048]{1,0:T(8,128)(2,1)S(1)} %collective-permute-done.1, bf16[128,2048]{1,0:T(8,128)(2,1)S(1)} %collective-permute-done, bf16[4096,2048]{1,0:T(8,128)(2,1)} %bitcast.42, bf16[512,4096]{1,0:T(8,128)(2,1)} %bitcast.47, ...), kind=kOutput, calls=%fused_computation.21 | convolution fusion | flops 2149842944 | bytes 19922948 | tf_op jit(solution)/shard_map/dot_general | solution.py:129
  (37 shorter events, 3.3 us)
Async XLA Ops:
  7.2 96.8 %copy-start = (f32[2048,8]{0,1:T(8,128)S(1)}, f32[2048,8]{0,1:T(8,128)}, u32[]{:S(2)}) copy-start(f32[2048,8]{0,1:T(8,128)} %param.11) | copy-start | bytes 196612
  7.2 95.0 %copy-start.8 = (s32[8]{0:T(128)S(1)}, s32[8]{0:T(128)}, u32[]{:S(2)}) copy-start(s32[8]{0:T(128)} %param.16) | copy-start | bytes 100
  7.2 96.2 %copy-start.4 = (bf16[512,2048]{1,0:T(8,128)(2,1)S(1)}, bf16[512,2048]{1,0:T(8,128)(2,1)}, u32[]{:S(2)}) copy-start(bf16[512,2048]{1,0:T(8,128)(2,1)} %param.9) | copy-start | bytes 6291460
  7.2 96.7 %copy-start.7 = (f32[2048]{0:T(1024)S(1)}, f32[2048]{0:T(1024)}, u32[]{:S(2)}) copy-start(f32[2048]{0:T(1024)} %param.10) | copy-start | bytes 24580
  7.2 94.2 %all-gather.4.cloned.1.call-start = ((), (), s32[]{:S(2)}) async-start(), calls=%async_computation | async-start | bytes 18874368 | tf_op jit(solution)/shard_map/all_gather | solution.py:244
  7.9 135.7 %all-gather.6.cloned.1.call-start = ((), (), s32[]{:S(2)}) async-start(), calls=%async_computation.1 | async-start | bytes 4718592 | tf_op jit(solution)/shard_map/all_gather | solution.py:248
  101.4 4.3 %copy-start.6 = (s32[512,2]{0,1:T(2,128)S(1)}, s32[512,2]{0,1:T(2,128)}, u32[]{:S(2)}) copy-start(s32[512,2]{0,1:T(2,128)} %param.15) | copy-start | bytes 12292
  101.4 133.6 %all-gather.8.cloned.1.call-start = ((), (), s32[]{:S(2)}) async-start(), calls=%async_computation.2 | async-start | bytes 18874368 | tf_op jit(solution)/shard_map/all_gather | solution.py:249
  141.1 2.6 copy-start.5
  235.1 10.9 %copy-start.2 = (bf16[8,512,2048]{2,1,0:T(8,128)(2,1)S(1)}, bf16[8,512,2048]{2,1,0:T(8,128)(2,1)}, u32[]{:S(2)}) copy-start(bf16[8,512,2048]{2,1,0:T(8,128)(2,1)} %all-gather.8.cloned.1.call-done) | copy-start | bytes 50331652
  235.1 12.0 %copy-start.3 = (bf16[64,8,8,512]{3,1,2,0:T(8,128)(2,1)S(1)}, bf16[64,8,8,512]{3,1,2,0:T(8,128)(2,1)}, u32[]{:S(2)}) copy-start(bf16[64,8,8,512]{3,1,2,0:T(8,128)(2,1)} %copy.32) | copy-start | bytes 12582916
  243.7 13.9 %collective-permute-start = (bf16[128,2048]{1,0:T(8,128)(2,1)S(1)}, bf16[128,2048]{1,0:T(8,128)(2,1)S(1)}, u32[]{:S(2)}, u32[]{:S(2)}) collective-permute-start(bf16[128,2048]{1,0:T(8,128)(2,1)S(1)} %convolution_convert_fusion.3), channel_id=1, source_target_pairs={{0,1},{1,2},{2,3},{3,0},{4,5},{5,6},{6,7},{7,4},{8,9},{9,10},{10,1... | collective-permute-start | bytes 1572872 | tf_op jit(solution)/shard_map/ppermute | solution.py:131
  250.4 39.4 %collective-permute-start.1 = (bf16[128,2048]{1,0:T(8,128)(2,1)}, bf16[128,2048]{1,0:T(8,128)(2,1)S(1)}, u32[]{:S(2)}, u32[]{:S(2)}) collective-permute-start(bf16[128,2048]{1,0:T(8,128)(2,1)} %convolution_convert_fusion.2), channel_id=1, source_target_pairs={{0,2},{1,3},{2,0},{3,1},{4,6},{5,7},{6,4},{7,5},{8,10},{9,11},{10,... | collective-permute-start | bytes 1572872 | tf_op jit(solution)/shard_map/ppermute | solution.py:131
  255.8 36.4 %collective-permute-start.2 = (bf16[128,2048]{1,0:T(8,128)(2,1)}, bf16[128,2048]{1,0:T(8,128)(2,1)}, u32[]{:S(2)}, u32[]{:S(2)}) collective-permute-start(bf16[128,2048]{1,0:T(8,128)(2,1)} %convolution_convert_fusion.1), channel_id=1, source_target_pairs={{0,3},{1,0},{2,1},{3,2},{4,7},{5,4},{6,5},{7,6},{8,11},{9,8},{10,9... | collective-permute-start | bytes 1572872 | tf_op jit(solution)/shard_map/ppermute | solution.py:131
  292.3 9.4 %copy-start.1 = (f32[2048,8]{0,1:T(8,128)S(1)}, f32[2048,8]{0,1:T(8,128)}, u32[]{:S(2)}) copy-start(f32[2048,8]{0,1:T(8,128)} %param.11) | copy-start | bytes 196612
Sparse Core Ops, SparseCore 0:
  10.0 91.4 all-gather.3
  103.3 36.7 all-gather.5
  141.9 93.1 all-gather.7

commit v4 on v3

--- a/solution.py
+++ b/solution.py
@@ -118,21 +118,27 @@
     return (own + rightward + leftward).astype(parts.dtype)
 
 
-def exchange_reduce(rows, weight, axis):
+def exchange_parts(rows, weight, axis):
     count = lax.axis_size(axis)
     me = lax.axis_index(axis)
     span = rows.shape[0] // count
-    total = None
+    parts = []
     for shift in list(range(1, count)) + [0]:
         target = lax.rem(me + shift, count)
         block_rows = lax.dynamic_slice_in_dim(rows, target * span, span, 0)
-        part = jnp.dot(block_rows, weight, preferred_element_type=jnp.float32).astype(jnp.bfloat16)
-        if shift:
-            part = lax.ppermute(part, axis, [(src, (src + shift) % count) for src in range(count)])
-        part = part.astype(jnp.float32)
-        total = part if total is None else total + part
+        parts.append(
+            jnp.dot(block_rows, weight, preferred_element_type=jnp.float32).astype(jnp.bfloat16)
+        )
+    return parts
+
+
+def exchange_finish(parts, axis):
+    count = lax.axis_size(axis)
+    total = parts[-1].astype(jnp.float32)
+    for shift, part in zip(range(1, count), parts):
+        moved = lax.ppermute(part, axis, [(src, (src + shift) % count) for src in range(count)])
+        total = total + moved.astype(jnp.float32)
     return total.astype(jnp.bfloat16)
-
 
 def attention_kernel(
     length_ref, q_ref, cache_ref, fresh_ref, out_ref, peak_ref, total_ref, accum_ref, *, cache_blocks
@@ -246,7 +252,11 @@
         (query_full, kv_weight, out_weight)
     )
     kv_full = lax.all_gather(kv_weight, "req", axis=0, tiled=True)
-    out_full = lax.all_gather(out_weight, "req", axis=2, tiled=True)
+    half = out_weight.shape[2] // 2
+    out_halves = [
+        lax.all_gather(piece, "req", axis=2, tiled=True)
+        for piece in (out_weight[:, :, :half], out_weight[:, :, half:])
+    ]
     projected = jnp.dot(normed, kv_full, preferred_element_type=jnp.float32)
     query_all = jnp.einsum(
         "tc,ecn->etn", normed, query_full, preferred_element_type=jnp.float32
@@ -270,8 +280,19 @@
     token_hot = jnp.transpose(one_hot, (1, 0, 2))
     mixture = jnp.sum(jnp.where(token_hot[..., None], weighted[:, :, None, :], 0), axis=0)
     mixture_flat = mixture.reshape(tok_count, experts * local_heads * head_dim)
-    flat_piece = out_full.reshape(experts * local_heads * head_dim, out_full.shape[2])
-    result = exchange_reduce(mixture_flat, flat_piece, "head")
+    flat_halves = [
+        piece.reshape(experts * local_heads * head_dim, piece.shape[2]) for piece in out_halves
+    ]
+    first_parts = exchange_parts(mixture_flat, flat_halves[0], "head")
+    _, second_weight = lax.optimization_barrier((first_parts, flat_halves[1]))
+    results = [
+        exchange_finish(first_parts, "head"),
+        exchange_finish(exchange_parts(mixture_flat, second_weight, "head"), "head"),
+    ]
+    column_blocks = out_halves[0].shape[2] // half
+    result = jnp.stack(
+        [part.reshape(part.shape[0], column_blocks, half) for part in results], axis=2
+    ).reshape(results[0].shape[0], 2 * half * column_blocks)
     return (result, fresh_kv[None])
 
 

time: 309 us -> 303 us (0.981)
  Pallas kernels: 40.4 us -> 30.5 us
  local copies, waits for them, and re-layouts: 21.5 us -> 29.1 us
  matrix products: 45.7 us -> 39.7 us
    ppermute x3 -> x6, waiting for transfers between devices: 34.8 us -> 19.6 us  [exchange_finish(): lax.ppermute(part, axis, [(src, (src + shift) % count) for src in range(c...]
    all_gather x1 -> x2, waiting for transfers between devices: 27.1 us -> 40.5 us  [shards(): lax.all_gather(piece, 'req', axis=2, tiled=True)]
    pallas_call x1, Pallas kernels: 40.4 us -> 30.5 us  [attend(): pl.pallas_call(functools.partial(attention_kernel, cache_blocks=cache_blo...]
    dot_general x4 -> x8, matrix products: 24.5 us -> 18 us  [exchange_parts(): jnp.dot(block_rows, weight, preferred_element_type=jnp.float32)]
    ppermute x3 -> x6, starting transfers between devices: 3.65 us -> 6.2 us  [exchange_finish(): lax.ppermute(part, axis, [(src, (src + shift) % count) for src in range(c...]
    unnamed x22 -> x28, local copies, waits for them, and re-layouts: 9.34 us -> 11.9 us
  transfers between devices with their start and end apart: 6 -> 10, of which waited for: 4 -> 5; matrix products, arithmetic and copies ran while one was open for 24% -> 29% of each run, Pallas kernels for 13% -> 10%
where the time goes in v4:
time: 303 us; the launch traced here: 302 us
  waiting for transfers between devices  155 us (51%)
  matrix products  39.7 us (13%)
  Pallas kernels  30.5 us (10%)
  local copies, waits for them, and re-layouts  29.1 us (10%)
  other arithmetic  27.7 us (9%)
  between operations  14.1 us (5%)
  starting transfers between devices  6.36 us (2%)
    all_gather x1, waiting for transfers between devices, shards(): query_full = lax.all_gather(query_weight, 'req', axis=1, tiled=True)  93.4 us
    all_gather x2, waiting for transfers between devices, shards(): lax.all_gather(piece, 'req', axis=2, tiled=True)  40.5 us
    pallas_call x1, Pallas kernels, attend(): pl.pallas_call(functools.partial(attention_kernel, cache_blocks=cache_blo...  30.5 us
    ppermute x6, waiting for transfers between devices, exchange_finish(): lax.ppermute(part, axis, [(src, (src + shift) % count) for src in range(c...  19.6 us
    dot_general x8, matrix products, exchange_parts(): jnp.dot(block_rows, weight, preferred_element_type=jnp.float32)  18 us
    dot_general x1, matrix products, shards(): jnp.einsum('tc,ecn->etn', normed, query_full, preferred_element_type=jnp....  15.1 us
    unnamed x28, local copies, waits for them, and re-layouts  11.9 us
    transpose x1, local copies, waits for them, and re-layouts, shards(): jnp.einsum('tc,ecn->etn', normed, query_full, preferred_element_type=jnp....  9.29 us
  transfers between devices with their start and end apart: 10, of which 5 were waited for; matrix products, arithmetic and copies ran while one was open for 29% of the time, Pallas kernels for 10%

profile of v4, /device:TPU:11, one launch (start us, length us, event | category | flops | bytes accessed | tf_op | source)
XLA Modules:
  0.0 302.3 jit_solution(12186538815554253820)
XLA Ops:
  8.0 93.4 %all-gather.5.cloned.1.call-done = bf16[8,2048,512]{2,1,0:T(8,128)(2,1)} async-done(((bf16[8,256,512]{2,1,0:T(8,128)(2,1)}), bf16[8,2048,512]{2,1,0:T(8,128)(2,1)}) %all-gather.5.cloned.1.call-update) | async-done | bytes 16777232 | tf_op jit(solution)/shard_map/all_gather | solution.py:250
  101.5 3.1 %fusion.31 = (bf16[8,512,128]{2,1,0:T(8,128)(2,1)}, bf16[8,512,128]{2,1,0:T(8,128)(2,1)}) fusion(bf16[8,512,256]{2,1,0:T(8,128)(2,1)} %param.14), kind=kLoop, calls=%fused_computation.67 | loop fusion | bytes 4194304 | tf_op jit(solution)/shard_map/slice | solution.py:258
  107.0 1.8 fusion.29
  110.2 15.1 %convolution_bitcast_fusion = f32[8,512,512]{1,2,0:T(8,128)} fusion(bf16[8,2048,512]{2,1,0:T(8,128)(2,1)} %all-gather.5.cloned.1.call-done, bf16[512,2048]{1,0:T(8,128)(2,1)S(1)} %copy-done.6, f32[2048]{0:T(1024)S(1)} %copy-done.9, f32[512]{0:T(512)S(1)} %add_rsqrt_fusion), kind=kOutput, calls=%fused_computation.7 | convolution fusion | flops 8594128896 | bytes 27273216 | tf_op jit(solution)/shard_map/tc,ecn->etn/dot_general | solution.py:261
  125.2 9.3 %copy.25 = f32[8,512,512]{2,1,0:T(8,128)} copy(f32[8,512,512]{1,2,0:T(8,128)} %convolution_bitcast_fusion) | data formatting | bytes 16777216 | tf_op jit(solution)/shard_map/tc,ecn->etn/transpose | solution.py:261
  134.5 6.4 %select_reduce_fusion = f32[2,512,512]{2,1,0:T(8,128)} fusion(f32[8,512,512]{2,1,0:T(8,128)} %copy.25, pred[2,8,512]{2,1,0:T(8,128)(4,1)S(1)} %iota_compare_fusion.1), kind=kLoop, calls=%fused_computation | loop fusion | flops 7864320 | bytes 10493952 | tf_op jit(solution)/shard_map/reduce_sum | solution.py:273
  140.9 1.9 reshape.248
  142.8 1.7 subtract_convert_fusion
  144.6 1.4 pad_maximum_fusion
  147.2 4.9 %fusion.26 = f32[512,1024]{0,1:T(8,128)S(1)} fusion(bf16[2048,1024]{1,0:T(8,128)(2,1)} %all-gather.7.cloned.1.call-done, bf16[512,2048]{1,0:T(8,128)(2,1)S(1)} %copy-done.7, f32[2048]{0:T(1024)S(1)} %copy-done.9, f32[512]{0:T(512)S(1)} %add_rsqrt_fusion), kind=kOutput, calls=%fused_computation.65 | convolution fusion | flops 2151677952 | bytes 8398848 | tf_op jit(solution)/shard_map/dot_general | solution.py:260
  153.4 1.3 copy.33
  155.1 1.4 pad_maximum_fusion.1.fresh_ref
  156.6 30.5 %shard_map.104 = f32[1024,512]{1,0:T(8,128)} custom-call(s32[1]{0:T(128)} %bitcast.2.length_ref, bf16[1024,512]{1,0:T(8,128)(2,1)} %bitcast.82, bf16[4,2048,256]{2,1,0:T(8,128)(2,1)} %bitcast.87, bf16[4,512,256]{2,1,0:T(8,128)(2,1)} %pad_maximum_fusion.1.fresh_ref), custom_call_target="tpu_custom_call" | custom-call | flops 5368709120 | bytes 8388608 | tf_op jit(solution)/shard_map/pallas_call | solution.py:216
  187.1 1.8 multiply_convert_fusion
  188.9 8.6 %select_reduce_fusion.1 = bf16[512,8,512]{2,1,0:T(8,128)(2,1)S(1)} fusion(pred[2,512,8]{2,1,0:T(8,128)(4,1)S(1)} %iota_compare_fusion, bf16[2,512,512]{2,1,0:T(8,128)(2,1)S(1)} %multiply_convert_fusion), kind=kLoop, calls=%fused_computation.1 | loop fusion | flops 6291456 | bytes 5251072 | tf_op jit(solution)/shard_map/reduce_sum | solution.py:281
  197.5 4.2 %copy.35 = bf16[64,8,8,512]{3,1,2,0:T(8,128)(2,1)} copy(bf16[64,8,8,512]{3,2,1,0:T(8,128)(2,1)S(1)} %bitcast.72) | data formatting | bytes 8388608
  201.7 5.1 %convolution_convert_fusion.4 = bf16[128,1024]{1,0:T(8,128)(2,1)S(1)} fusion(bf16[4096,1024]{1,0:T(8,128)(2,1)} %bitcast.56, bf16[512,4096]{1,0:T(8,128)(2,1)} %bitcast.64, s32[]{:T(128)S(6)} %select_n.39), kind=kOutput, calls=%fused_computation.17 | convolution fusion | flops 1073872896 | bytes 9699332 | tf_op jit(solution)/shard_map/dot_general | solution.py:130
  208.1 1.6 copy-done.4
  209.7 1.3 convolution_convert_fusion.5
  211.0 2.2 collective-permute-start.1
  213.2 1.3 convolution_convert_fusion.6
  214.5 1.3 convolution_convert_fusion.7
  215.8 40.5 %all-gather.11.cloned.1.call-done = bf16[8,512,1024]{2,1,0:T(8,128)(2,1)} async-done(((bf16[8,512,128]{2,1,0:T(8,128)(2,1)}), bf16[8,512,1024]{2,1,0:T(8,128)(2,1)}) %all-gather.11.cloned.1.call-update) | async-done | bytes 8388624 | tf_op jit(solution)/shard_map/all_gather | solution.py:257
  256.3 5.1 %convolution_convert_fusion.2 = bf16[128,1024]{1,0:T(8,128)(2,1)S(1)} fusion(bf16[4096,1024]{1,0:T(8,128)(2,1)} %bitcast.60, bf16[512,4096]{1,0:T(8,128)(2,1)} %bitcast.65, s32[]{:T(128)S(6)} %select_n.37), kind=kOutput, calls=%fused_computation.14 | convolution fusion | flops 1073872896 | bytes 9699332 | tf_op jit(solution)/shard_map/dot_general | solution.py:130
  264.9 1.3 convolution_convert_fusion
  266.1 1.3 collective-permute-start.3
  269.8 1.4 pad_maximum_fusion.2
  271.2 1.3 fusion.13
  272.6 1.3 collective-permute-done.3
  273.8 15.9 %collective-permute-done.4 = bf16[128,1024]{1,0:T(8,128)(2,1)S(1)} collective-permute-done((bf16[128,1024]{1,0:T(8,128)(2,1)S(1)}, bf16[128,1024]{1,0:T(8,128)(2,1)S(1)}, u32[]{:S(2)}, u32[]{:S(2)}) %collective-permute-start.4) | collective-permute-done | bytes 262176 | tf_op jit(solution)/shard_map/ppermute | solution.py:139
  289.7 2.5 collective-permute-done.5
  292.2 1.4 fusion.14
  (61 shorter events, 16.6 us)
Async XLA Ops:
  7.2 99.9 %copy-start = (f32[2048,8]{0,1:T(8,128)S(1)}, f32[2048,8]{0,1:T(8,128)}, u32[]{:S(2)}) copy-start(f32[2048,8]{0,1:T(8,128)} %param.11) | copy-start | bytes 196612
  7.2 98.0 %copy-start.10 = (s32[8]{0:T(128)S(1)}, s32[8]{0:T(128)}, u32[]{:S(2)}) copy-start(s32[8]{0:T(128)} %param.16) | copy-start | bytes 100
  7.2 99.3 %copy-start.6 = (bf16[512,2048]{1,0:T(8,128)(2,1)S(1)}, bf16[512,2048]{1,0:T(8,128)(2,1)}, u32[]{:S(2)}) copy-start(bf16[512,2048]{1,0:T(8,128)(2,1)} %param.9) | copy-start | bytes 6291460
  7.2 94.2 %all-gather.5.cloned.1.call-start = ((), (), s32[]{:S(2)}) async-start(), calls=%async_computation | async-start | bytes 18874368 | tf_op jit(solution)/shard_map/all_gather | solution.py:250
  7.9 139.2 %all-gather.7.cloned.1.call-start = ((), (), s32[]{:S(2)}) async-start(), calls=%async_computation.1 | async-start | bytes 4718592 | tf_op jit(solution)/shard_map/all_gather | solution.py:254
  101.4 5.6 %copy-start.9 = (f32[2048]{0:T(1024)S(1)}, f32[2048]{0:T(1024)}, u32[]{:S(2)}) copy-start(f32[2048]{0:T(1024)} %param.10) | copy-start | bytes 24580
  101.4 100.3 %all-gather.9.cloned.1.call-start = ((), (), s32[]{:S(2)}) async-start(), calls=%async_computation.2 | async-start | bytes 9437184 | tf_op jit(solution)/shard_map/all_gather | solution.py:257
  104.6 4.3 %copy-start.8 = (s32[512,2]{0,1:T(2,128)S(1)}, s32[512,2]{0,1:T(2,128)}, u32[]{:S(2)}) copy-start(s32[512,2]{0,1:T(2,128)} %param.15) | copy-start | bytes 12292
  104.6 151.7 %all-gather.11.cloned.1.call-start = ((), (), s32[]{:S(2)}) async-start(), calls=%async_computation.3 | async-start | bytes 9437184 | tf_op jit(solution)/shard_map/all_gather | solution.py:257
  144.6 2.6 copy-start.7
  201.7 6.4 %copy-start.2 = (bf16[8,512,1024]{2,1,0:T(8,128)(2,1)S(1)}, bf16[8,512,1024]{2,1,0:T(8,128)(2,1)}, u32[]{:S(2)}) copy-start(bf16[8,512,1024]{2,1,0:T(8,128)(2,1)} %all-gather.9.cloned.1.call-done) | copy-start | bytes 25165828
  201.7 8.0 %copy-start.4 = (bf16[64,8,8,512]{3,1,2,0:T(8,128)(2,1)S(1)}, bf16[64,8,8,512]{3,1,2,0:T(8,128)(2,1)}, u32[]{:S(2)}) copy-start(bf16[64,8,8,512]{3,1,2,0:T(8,128)(2,1)} %copy.35) | copy-start | bytes 12582916
  206.8 61.7 %collective-permute-start.2 = (bf16[128,1024]{1,0:T(8,128)(2,1)S(1)}, bf16[128,1024]{1,0:T(8,128)(2,1)}, u32[]{:S(2)}, u32[]{:S(2)}) collective-permute-start(bf16[128,1024]{1,0:T(8,128)(2,1)S(1)} %convolution_convert_fusion.4), channel_id=1, source_target_pairs={{0,3},{1,0},{2,1},{3,2},{4,7},{5,4},{6,5},{7,6},{8,11},{9,8},{10,9... | collective-permute-start | bytes 786440 | tf_op jit(solution)/shard_map/ppermute | solution.py:139
  211.0 60.2 %collective-permute-start.1 = (bf16[128,1024]{1,0:T(8,128)(2,1)S(1)}, bf16[128,1024]{1,0:T(8,128)(2,1)}, u32[]{:S(2)}, u32[]{:S(2)}) collective-permute-start(bf16[128,1024]{1,0:T(8,128)(2,1)S(1)} %convolution_convert_fusion.5), channel_id=1, source_target_pairs={{0,2},{1,3},{2,0},{3,1},{4,6},{5,7},{6,4},{7,5},{8,10},{9,11},{10,... | collective-permute-start | bytes 786440 | tf_op jit(solution)/shard_map/ppermute | solution.py:139
  214.4 56.8 %collective-permute-start = (bf16[128,1024]{1,0:T(8,128)(2,1)S(1)}, bf16[128,1024]{1,0:T(8,128)(2,1)}, u32[]{:S(2)}, u32[]{:S(2)}) collective-permute-start(bf16[128,1024]{1,0:T(8,128)(2,1)S(1)} %convolution_convert_fusion.6), channel_id=1, source_target_pairs={{0,1},{1,2},{2,3},{3,0},{4,5},{5,6},{6,7},{7,4},{8,9},{9,10},{10,1... | collective-permute-start | bytes 786440 | tf_op jit(solution)/shard_map/ppermute | solution.py:139
  256.3 6.1 %copy-start.3 = (bf16[8,512,1024]{2,1,0:T(8,128)(2,1)S(1)}, bf16[8,512,1024]{2,1,0:T(8,128)(2,1)}, u32[]{:S(2)}) copy-start(bf16[8,512,1024]{2,1,0:T(8,128)(2,1)} %all-gather.11.cloned.1.call-done) | copy-start | bytes 25165828
  256.3 7.3 %copy-start.5 = (bf16[64,8,8,512]{3,1,2,0:T(8,128)(2,1)S(1)}, bf16[64,8,8,512]{3,1,2,0:T(8,128)(2,1)}, u32[]{:S(2)}) copy-start(bf16[64,8,8,512]{3,1,2,0:T(8,128)(2,1)} %copy.35) | copy-start | bytes 12582916
  266.1 7.7 %collective-permute-start.3 = (bf16[128,1024]{1,0:T(8,128)(2,1)S(1)}, bf16[128,1024]{1,0:T(8,128)(2,1)S(1)}, u32[]{:S(2)}, u32[]{:S(2)}) collective-permute-start(bf16[128,1024]{1,0:T(8,128)(2,1)S(1)} %convolution_convert_fusion.2), channel_id=1, source_target_pairs={{0,1},{1,2},{2,3},{3,0},{4,5},{5,6},{6,7},{7,4},{8,9},{9,10},{10,1... | collective-permute-start | bytes 786440 | tf_op jit(solution)/shard_map/ppermute | solution.py:139
  267.4 22.3 %collective-permute-start.4 = (bf16[128,1024]{1,0:T(8,128)(2,1)S(1)}, bf16[128,1024]{1,0:T(8,128)(2,1)S(1)}, u32[]{:S(2)}, u32[]{:S(2)}) collective-permute-start(bf16[128,1024]{1,0:T(8,128)(2,1)S(1)} %convolution_convert_fusion.1), channel_id=1, source_target_pairs={{0,2},{1,3},{2,0},{3,1},{4,6},{5,7},{6,4},{7,5},{8,10},{9,11},{10,... | collective-permute-start | bytes 786440 | tf_op jit(solution)/shard_map/ppermute | solution.py:139
  268.5 23.7 %collective-permute-start.5 = (bf16[128,1024]{1,0:T(8,128)(2,1)S(1)}, bf16[128,1024]{1,0:T(8,128)(2,1)S(1)}, u32[]{:S(2)}, u32[]{:S(2)}) collective-permute-start(bf16[128,1024]{1,0:T(8,128)(2,1)S(1)} %convolution_convert_fusion), channel_id=1, source_target_pairs={{0,3},{1,0},{2,1},{3,2},{4,7},{5,4},{6,5},{7,6},{8,11},{9,8},{10,9... | collective-permute-start | bytes 786440 | tf_op jit(solution)/shard_map/ppermute | solution.py:139
  292.2 3.6 %copy-start.1 = (f32[2048,8]{0,1:T(8,128)S(1)}, f32[2048,8]{0,1:T(8,128)}, u32[]{:S(2)}) copy-start(f32[2048,8]{0,1:T(8,128)} %param.11) | copy-start | bytes 196612
Sparse Core Ops, SparseCore 0:
  9.9 91.4 all-gather.4
  103.3 36.7 all-gather.6
  141.9 55.9 all-gather.8
  200.2 56.0 all-gather.10

commit v5 on v4

--- a/solution.py
+++ b/solution.py
@@ -226,6 +226,20 @@
             bytes_accessed=2 * (cache.size + fresh.size + queries.size) + 4 * queries.size,
         ),
     )(jnp.reshape(length, (1,)).astype(jnp.int32), queries, cache, fresh)
+
+
+def xor_gather(block, axis):
+    count = lax.axis_size(axis)
+    me = lax.axis_index(axis)
+    if count & (count - 1):
+        return lax.all_gather(block, axis, axis=0, tiled=True)
+    arrived = [block] + [
+        lax.ppermute(block, axis, [(src, src ^ step) for src in range(count)])
+        for step in range(1, count)
+    ]
+    order = jnp.bitwise_xor(me, jnp.arange(count))
+    stacked = jnp.take(jnp.stack(arrived), order, axis=0)
+    return stacked.reshape(count * block.shape[0], *block.shape[1:])
 
 
 def shards(
@@ -251,7 +265,7 @@
     query_full, kv_weight, out_weight = lax.optimization_barrier(
         (query_full, kv_weight, out_weight)
     )
-    kv_full = lax.all_gather(kv_weight, "req", axis=0, tiled=True)
+    kv_full = xor_gather(kv_weight, "req")
     half = out_weight.shape[2] // 2
     out_halves = [
         lax.all_gather(piece, "req", axis=2, tiled=True)

time: 303 us -> 341 us (1.13)
  Pallas kernels: 30.5 us -> 60.5 us
  waiting for transfers between devices: 155 us -> 132 us
  local copies, waits for them, and re-layouts: 29.1 us -> 49.6 us
  starting transfers between devices: 6.36 us -> 13.4 us
    all_gather x2, waiting for transfers between devices: 40.5 us -> 0.02 us  [shards(): lax.all_gather(piece, 'req', axis=2, tiled=True)]
    pallas_call x1, Pallas kernels: 30.5 us -> 60.5 us  [attend(): pl.pallas_call(functools.partial(attention_kernel, cache_blocks=cache_blo...]
    ppermute x0 -> x7, waiting for transfers between devices: none -> 27 us  [xor_gather(): lax.ppermute(block, axis, [(src, src ^ step) for src in range(count)])]
    ppermute x6, waiting for transfers between devices: 19.6 us -> 9.92 us  [exchange_finish(): lax.ppermute(part, axis, [(src, (src + shift) % count) for src in range(c...]
    unnamed x28 -> x35, local copies, waits for them, and re-layouts: 11.9 us -> 20.3 us
    dot_general x0 -> x1, local copies, waits for them, and re-layouts: none -> 6.8 us  [shards(): projected = jnp.dot(normed, kv_full, preferred_element_type=jnp.float32)]
    ppermute x0 -> x7, starting transfers between devices: none -> 6.64 us  [xor_gather(): lax.ppermute(block, axis, [(src, src ^ step) for src in range(count)])]
    gather x0 -> x1, local copies, waits for them, and re-layouts: none -> 5.01 us  [xor_gather(): stacked = jnp.take(jnp.stack(arrived), order, axis=0)]
  transfers between devices with their start and end apart: 10 -> 16, of which waited for: 5 -> 6; matrix products, arithmetic and copies ran while one was open for 29% -> 32% of each run, Pallas kernels for 10% -> 18%
where the time goes in v5:
time: 341 us; the launch traced here: 339 us
  waiting for transfers between devices  132 us (39%)
  Pallas kernels  60.5 us (18%)
  local copies, waits for them, and re-layouts  49.6 us (15%)
  matrix products  39.2 us (11%)
  other arithmetic  29.9 us (9%)
  between operations  14.2 us (4%)
  starting transfers between devices  13.4 us (4%)
    all_gather x1, waiting for transfers between devices, shards(): query_full = lax.all_gather(query_weight, 'req', axis=1, tiled=True)  93.4 us
    pallas_call x1, Pallas kernels, attend(): pl.pallas_call(functools.partial(attention_kernel, cache_blocks=cache_blo...  60.5 us
    ppermute x7, waiting for transfers between devices, xor_gather(): lax.ppermute(block, axis, [(src, src ^ step) for src in range(count)])  27 us
    unnamed x35, local copies, waits for them, and re-layouts  20.3 us
    dot_general x8, matrix products, exchange_parts(): jnp.dot(block_rows, weight, preferred_element_type=jnp.float32)  17.9 us
    dot_general x1, matrix products, shards(): jnp.einsum('tc,ecn->etn', normed, query_full, preferred_element_type=jnp....  14.9 us
    ppermute x6, waiting for transfers between devices, exchange_finish(): lax.ppermute(part, axis, [(src, (src + shift) % count) for src in range(c...  9.92 us
    transpose x1, local copies, waits for them, and re-layouts, shards(): jnp.einsum('tc,ecn->etn', normed, query_full, preferred_element_type=jnp....  9.17 us
  transfers between devices with their start and end apart: 16, of which 6 were waited for; matrix products, arithmetic and copies ran while one was open for 32% of the time, Pallas kernels for 18%

profile of v5, /device:TPU:11, one launch (start us, length us, event | category | flops | bytes accessed | tf_op | source)
XLA Modules:
  0.0 338.6 jit_solution(10961089581951281693)
XLA Ops:
  8.0 93.4 %all-gather.4.cloned.1.call-done = bf16[8,2048,512]{2,1,0:T(8,128)(2,1)} async-done(((bf16[8,256,512]{2,1,0:T(8,128)(2,1)}), bf16[8,2048,512]{2,1,0:T(8,128)(2,1)}) %all-gather.4.cloned.1.call-update) | async-done | bytes 16777232 | tf_op jit(solution)/shard_map/all_gather | solution.py:264
  101.4 3.1 fusion.36
  107.3 1.8 fusion.34
  111.0 1.6 collective-permute-start.2
  114.2 14.9 %convolution_bitcast_fusion = f32[8,512,512]{1,2,0:T(8,128)} fusion(bf16[8,2048,512]{2,1,0:T(8,128)(2,1)} %all-gather.4.cloned.1.call-done, bf16[512,2048]{1,0:T(8,128)(2,1)S(1)} %copy-done.6, f32[2048]{0:T(1024)S(1)} %copy-done.10, f32[512]{0:T(512)S(1)} %add_rsqrt_fusion), kind=kOutput, calls=%fused_computation.11 | convolution fusion | flops 8594128896 | bytes 27273216 | tf_op jit(solution)/shard_map/tc,ecn->etn/dot_general | solution.py:275
  129.1 9.2 %copy.20 = f32[8,512,512]{2,1,0:T(8,128)} copy(f32[8,512,512]{1,2,0:T(8,128)} %convolution_bitcast_fusion) | data formatting | bytes 16777216 | tf_op jit(solution)/shard_map/tc,ecn->etn/transpose | solution.py:275
  138.3 6.3 %select_reduce_fusion = f32[2,512,512]{2,1,0:T(8,128)} fusion(f32[8,512,512]{2,1,0:T(8,128)} %copy.20, pred[2,8,512]{2,1,0:T(8,128)(4,1)S(1)} %iota_compare_fusion.1), kind=kLoop, calls=%fused_computation.1 | loop fusion | flops 7864320 | bytes 10493952 | tf_op jit(solution)/shard_map/reduce_sum | solution.py:287
  144.6 2.1 reshape.271
  146.7 1.5 subtract_convert_fusion
  152.3 1.9 bitcast_dynamic-update-slice_fusion.6
  154.2 2.3 collective-permute-start.6
  156.5 1.9 bitcast_dynamic-update-slice_fusion.5
  158.4 1.9 bitcast_dynamic-update-slice_fusion.4
  160.3 1.9 bitcast_dynamic-update-slice_fusion.3
  162.1 1.9 bitcast_dynamic-update-slice_fusion.2
  164.0 13.6 %collective-permute-done.5 = bf16[256,1024]{1,0:T(8,128)(2,1)S(1)} collective-permute-done((bf16[256,1024]{1,0:T(8,128)(2,1)S(1)}, bf16[256,1024]{1,0:T(8,128)(2,1)S(1)}, u32[]{:S(2)}, u32[]{:S(2)}) %collective-permute-start.5) | collective-permute-done | bytes 524320 | tf_op jit(solution)/shard_map/ppermute | solution.py:237
  178.4 13.4 %collective-permute-done.6 = bf16[256,1024]{1,0:T(8,128)(2,1)S(1)} collective-permute-done((bf16[256,1024]{1,0:T(8,128)(2,1)S(1)}, bf16[256,1024]{1,0:T(8,128)(2,1)S(1)}, u32[]{:S(2)}, u32[]{:S(2)}) %collective-permute-start.6) | collective-permute-done | bytes 524320 | tf_op jit(solution)/shard_map/ppermute | solution.py:237
  192.6 5.0 %gather_fusion = bf16[8,256,1024]{2,1,0:T(8,128)(2,1)} fusion(bf16[8,256,1024]{2,1,0:T(8,128)(2,1)} %bitcast_dynamic-update-slice_fusion, s32[1024]{0:T(1024)S(1)} %pad_clamp_fusion), kind=kCustom, calls=%fused_computation | custom fusion | bytes 8388640 | tf_op jit(solution)/shard_map/jit(_take)/gather | solution.py:241
  197.6 3.8 %bitcast_select_fusion = bf16[2048,1024]{1,0:T(8,128)(2,1)} fusion(bf16[8,256,1024]{2,1,0:T(8,128)(2,1)} %gather_fusion, pred[2048]{0:T(1024)(128)(4,1)S(1)} %broadcast_in_dim.103), kind=kLoop, calls=%fused_computation.8 | loop fusion | flops 2097152 | bytes 8390656 | tf_op jit(solution)/shard_map/jit(_take)/select_n | solution.py:241
  201.4 6.8 %copy.21 = bf16[1024,2048]{1,0:T(8,128)(2,1)} copy(bf16[1024,2048]{0,1:T(8,128)(2,1)} %bitcast.94) | data formatting | bytes 8388608 | tf_op jit(solution)/shard_map/dot_general | solution.py:274
  208.2 4.6 %fusion.3 = f32[512,4,2,128]{3,0,1,2:T(8,128)S(1)} fusion(bf16[4,2,128,2048]{3,2,1,0:T(8,128)(2,1)} %bitcast.99, bf16[512,2048]{1,0:T(8,128)(2,1)S(1)} %copy-done.7, f32[2048]{0:T(1024)S(1)} %copy-done.10, f32[512]{0:T(512)S(1)} %add_rsqrt_fusion), kind=kOutput, calls=%fused_computation.9 | convolution fusion | flops 2151677952 | bytes 8398848 | tf_op jit(solution)/shard_map/dot_general | solution.py:274
  213.5 1.5 pad_maximum_fusion.1.fresh_ref
  214.9 60.5 %shard_map.104 = f32[1024,512]{1,0:T(8,128)} custom-call(s32[1]{0:T(128)} %bitcast.2.length_ref, bf16[1024,512]{1,0:T(8,128)(2,1)} %bitcast.101, bf16[4,2048,256]{2,1,0:T(8,128)(2,1)} %bitcast.106, bf16[4,512,256]{2,1,0:T(8,128)(2,1)} %pad_maximum_fusion.1.fresh_ref), custom_call_target="tpu_custom_call" | custom-call | flops 5368709120 | bytes 8388608 | tf_op jit(solution)/shard_map/pallas_call | solution.py:216
  275.5 1.8 multiply_convert_fusion
  277.3 8.4 %select_reduce_fusion.1 = bf16[512,8,512]{2,1,0:T(8,128)(2,1)S(1)} fusion(pred[2,512,8]{2,1,0:T(8,128)(4,1)S(1)} %iota_compare_fusion, bf16[2,512,512]{2,1,0:T(8,128)(2,1)S(1)} %multiply_convert_fusion), kind=kLoop, calls=%fused_computation.2 | loop fusion | flops 6291456 | bytes 5251072 | tf_op jit(solution)/shard_map/reduce_sum | solution.py:295
  285.7 4.2 %copy.29 = bf16[64,8,8,512]{3,1,2,0:T(8,128)(2,1)} copy(bf16[64,8,8,512]{3,2,1,0:T(8,128)(2,1)S(1)} %bitcast.95) | data formatting | bytes 8388608
  289.9 5.1 %convolution_convert_fusion.4 = bf16[128,1024]{1,0:T(8,128)(2,1)S(1)} fusion(bf16[4096,1024]{1,0:T(8,128)(2,1)} %bitcast.78, bf16[512,4096]{1,0:T(8,128)(2,1)} %bitcast.86, s32[]{:T(128)S(6)} %select_n.63), kind=kOutput, calls=%fused_computation.22 | convolution fusion | flops 1073872896 | bytes 9699332 | tf_op jit(solution)/shard_map/dot_general | solution.py:130
  298.4 2.2 collective-permute-start.8
  303.8 5.1 %convolution_convert_fusion.2 = bf16[128,1024]{1,0:T(8,128)(2,1)S(1)} fusion(bf16[4096,1024]{1,0:T(8,128)(2,1)} %bitcast.82, bf16[512,4096]{1,0:T(8,128)(2,1)} %bitcast.87, s32[]{:T(128)S(6)} %select_n.61), kind=kOutput, calls=%fused_computation.19 | convolution fusion | flops 1073872896 | bytes 9699332 | tf_op jit(solution)/shard_map/dot_general | solution.py:130
  313.6 3.0 collective-permute-start.11
  318.8 6.7 %collective-permute-done.11 = bf16[128,1024]{1,0:T(8,128)(2,1)S(1)} collective-permute-done((bf16[128,1024]{1,0:T(8,128)(2,1)S(1)}, bf16[128,1024]{1,0:T(8,128)(2,1)S(1)}, u32[]{:S(2)}, u32[]{:S(2)}) %collective-permute-start.11) | collective-permute-done | bytes 262176 | tf_op jit(solution)/shard_map/ppermute | solution.py:139
  325.6 2.9 collective-permute-done.12
  (88 shorter events, 30.2 us)
Async XLA Ops:
  7.2 100.1 %copy-start = (f32[2048,8]{0,1:T(8,128)S(1)}, f32[2048,8]{0,1:T(8,128)}, u32[]{:S(2)}) copy-start(f32[2048,8]{0,1:T(8,128)} %param.11) | copy-start | bytes 196612
  7.2 98.2 %copy-start.11 = (s32[8]{0:T(128)S(1)}, s32[8]{0:T(128)}, u32[]{:S(2)}) copy-start(s32[8]{0:T(128)} %param.16) | copy-start | bytes 100
  7.2 99.5 %copy-start.6 = (bf16[512,2048]{1,0:T(8,128)(2,1)S(1)}, bf16[512,2048]{1,0:T(8,128)(2,1)}, u32[]{:S(2)}) copy-start(bf16[512,2048]{1,0:T(8,128)(2,1)} %param.9) | copy-start | bytes 6291460
  7.2 94.2 %all-gather.4.cloned.1.call-start = ((), (), s32[]{:S(2)}) async-start(), calls=%async_computation | async-start | bytes 18874368 | tf_op jit(solution)/shard_map/all_gather | solution.py:264
  7.9 99.3 %copy-start.10 = (f32[2048]{0:T(1024)S(1)}, f32[2048]{0:T(1024)}, u32[]{:S(2)}) copy-start(f32[2048]{0:T(1024)} %param.10) | copy-start | bytes 24580
  7.9 281.9 %all-gather.6.cloned.1.call-start = ((), (), s32[]{:S(2)}) async-start(), calls=%async_computation.1 | async-start | bytes 9437184 | tf_op jit(solution)/shard_map/all_gather | solution.py:271
  104.5 4.6 %copy-start.9 = (s32[512,2]{0,1:T(2,128)S(1)}, s32[512,2]{0,1:T(2,128)}, u32[]{:S(2)}) copy-start(s32[512,2]{0,1:T(2,128)} %param.15) | copy-start | bytes 12292
  104.5 5.9 %copy-start.8 = (bf16[256,1024]{1,0:T(8,128)(2,1)S(1)}, bf16[256,1024]{1,0:T(8,128)(2,1)}, u32[]{:S(2)}) copy-start(bf16[256,1024]{1,0:T(8,128)(2,1)} %param.12) | copy-start | bytes 1572868
  104.5 199.2 %all-gather.8.cloned.1.call-start = ((), (), s32[]{:S(2)}) async-start(), calls=%async_computation.2 | async-start | bytes 9437184 | tf_op jit(solution)/shard_map/all_gather | solution.py:271
  110.4 41.4 %collective-permute-start = (bf16[256,1024]{1,0:T(8,128)(2,1)S(1)}, bf16[256,1024]{1,0:T(8,128)(2,1)}, u32[]{:S(2)}, u32[]{:S(2)}) collective-permute-start(bf16[256,1024]{1,0:T(8,128)(2,1)S(1)} %copy-done.8), channel_id=1, source_target_pairs={{0,4},{4,0},{8,12},{12,8},{16,20},{20,16},{24,28},{28,24},{1,5},{5... | collective-permute-start | bytes 1572872 | tf_op jit(solution)/shard_map/ppermute | solution.py:237
  110.7 43.5 %collective-permute-start.1 = (bf16[256,1024]{1,0:T(8,128)(2,1)S(1)}, bf16[256,1024]{1,0:T(8,128)(2,1)}, u32[]{:S(2)}, u32[]{:S(2)}) collective-permute-start(bf16[256,1024]{1,0:T(8,128)(2,1)S(1)} %copy-done.8), channel_id=1, source_target_pairs={{0,8},{4,12},{8,0},{12,4},{16,24},{20,28},{24,16},{28,20},{1,9},{5... | collective-permute-start | bytes 1572872 | tf_op jit(solution)/shard_map/ppermute | solution.py:237
  111.0 47.4 %collective-permute-start.2 = (bf16[256,1024]{1,0:T(8,128)(2,1)S(1)}, bf16[256,1024]{1,0:T(8,128)(2,1)}, u32[]{:S(2)}, u32[]{:S(2)}) collective-permute-start(bf16[256,1024]{1,0:T(8,128)(2,1)S(1)} %copy-done.8), channel_id=1, source_target_pairs={{0,12},{4,8},{8,4},{12,0},{16,28},{20,24},{24,20},{28,16},{1,13},{... | collective-permute-start | bytes 1572872 | tf_op jit(solution)/shard_map/ppermute | solution.py:237
  112.6 47.7 %collective-permute-start.3 = (bf16[256,1024]{1,0:T(8,128)(2,1)S(1)}, bf16[256,1024]{1,0:T(8,128)(2,1)}, u32[]{:S(2)}, u32[]{:S(2)}) collective-permute-start(bf16[256,1024]{1,0:T(8,128)(2,1)S(1)} %copy-done.8), channel_id=1, source_target_pairs={{0,16},{4,20},{8,24},{12,28},{16,0},{20,4},{24,8},{28,12},{1,17},{... | collective-permute-start | bytes 1572872 | tf_op jit(solution)/shard_map/ppermute | solution.py:237
  112.9 49.3 %collective-permute-start.4 = (bf16[256,1024]{1,0:T(8,128)(2,1)S(1)}, bf16[256,1024]{1,0:T(8,128)(2,1)}, u32[]{:S(2)}, u32[]{:S(2)}) collective-permute-start(bf16[256,1024]{1,0:T(8,128)(2,1)S(1)} %copy-done.8), channel_id=1, source_target_pairs={{0,20},{4,16},{8,28},{12,24},{16,4},{20,0},{24,12},{28,8},{1,21},{... | collective-permute-start | bytes 1572872 | tf_op jit(solution)/shard_map/ppermute | solution.py:237
  151.8 25.8 %collective-permute-start.5 = (bf16[256,1024]{1,0:T(8,128)(2,1)S(1)}, bf16[256,1024]{1,0:T(8,128)(2,1)S(1)}, u32[]{:S(2)}, u32[]{:S(2)}) collective-permute-start(bf16[256,1024]{1,0:T(8,128)(2,1)S(1)} %copy-done.8), channel_id=1, source_target_pairs={{0,24},{4,28},{8,16},{12,20},{16,8},{20,12},{24,0},{28,4},{1,25},{... | collective-permute-start | bytes 1572872 | tf_op jit(solution)/shard_map/ppermute | solution.py:237
  154.2 37.6 %collective-permute-start.6 = (bf16[256,1024]{1,0:T(8,128)(2,1)S(1)}, bf16[256,1024]{1,0:T(8,128)(2,1)S(1)}, u32[]{:S(2)}, u32[]{:S(2)}) collective-permute-start(bf16[256,1024]{1,0:T(8,128)(2,1)S(1)} %copy-done.8), channel_id=1, source_target_pairs={{0,28},{4,24},{8,20},{12,16},{16,12},{20,8},{24,4},{28,0},{1,29},{... | collective-permute-start | bytes 1572872 | tf_op jit(solution)/shard_map/ppermute | solution.py:237
  201.4 6.8 %copy-start.7 = (bf16[512,2048]{1,0:T(8,128)(2,1)S(1)}, bf16[512,2048]{1,0:T(8,128)(2,1)}, u32[]{:S(2)}) copy-start(bf16[512,2048]{1,0:T(8,128)(2,1)} %param.9) | copy-start | bytes 6291460
  289.9 6.1 %copy-start.2 = (bf16[8,512,1024]{2,1,0:T(8,128)(2,1)S(1)}, bf16[8,512,1024]{2,1,0:T(8,128)(2,1)}, u32[]{:S(2)}) copy-start(bf16[8,512,1024]{2,1,0:T(8,128)(2,1)} %all-gather.6.cloned.1.call-done) | copy-start | bytes 25165828
  289.9 7.3 %copy-start.4 = (bf16[64,8,8,512]{3,1,2,0:T(8,128)(2,1)S(1)}, bf16[64,8,8,512]{3,1,2,0:T(8,128)(2,1)}, u32[]{:S(2)}) copy-start(bf16[64,8,8,512]{3,1,2,0:T(8,128)(2,1)} %copy.29) | copy-start | bytes 12582916
  295.0 21.7 %collective-permute-start.9 = (bf16[128,1024]{1,0:T(8,128)(2,1)S(1)}, bf16[128,1024]{1,0:T(8,128)(2,1)S(1)}, u32[]{:S(2)}, u32[]{:S(2)}) collective-permute-start(bf16[128,1024]{1,0:T(8,128)(2,1)S(1)} %convolution_convert_fusion.4), channel_id=1, source_target_pairs={{0,3},{1,0},{2,1},{3,2},{4,7},{5,4},{6,5},{7,6},{8,11},{9,8},{10,9... | collective-permute-start | bytes 786440 | tf_op jit(solution)/shard_map/ppermute | solution.py:139
  298.4 19.9 %collective-permute-start.8 = (bf16[128,1024]{1,0:T(8,128)(2,1)S(1)}, bf16[128,1024]{1,0:T(8,128)(2,1)S(1)}, u32[]{:S(2)}, u32[]{:S(2)}) collective-permute-start(bf16[128,1024]{1,0:T(8,128)(2,1)S(1)} %convolution_convert_fusion.5), channel_id=1, source_target_pairs={{0,2},{1,3},{2,0},{3,1},{4,6},{5,7},{6,4},{7,5},{8,10},{9,11},{10,... | collective-permute-start | bytes 786440 | tf_op jit(solution)/shard_map/ppermute | solution.py:139
  301.9 16.5 %collective-permute-start.7 = (bf16[128,1024]{1,0:T(8,128)(2,1)S(1)}, bf16[128,1024]{1,0:T(8,128)(2,1)S(1)}, u32[]{:S(2)}, u32[]{:S(2)}) collective-permute-start(bf16[128,1024]{1,0:T(8,128)(2,1)S(1)} %convolution_convert_fusion.6), channel_id=1, source_target_pairs={{0,1},{1,2},{2,3},{3,0},{4,5},{5,6},{6,7},{7,4},{8,9},{9,10},{10,1... | collective-permute-start | bytes 786440 | tf_op jit(solution)/shard_map/ppermute | solution.py:139
  303.8 6.1 %copy-start.3 = (bf16[8,512,1024]{2,1,0:T(8,128)(2,1)S(1)}, bf16[8,512,1024]{2,1,0:T(8,128)(2,1)}, u32[]{:S(2)}) copy-start(bf16[8,512,1024]{2,1,0:T(8,128)(2,1)} %all-gather.8.cloned.1.call-done) | copy-start | bytes 25165828
  303.8 7.3 %copy-start.5 = (bf16[64,8,8,512]{3,1,2,0:T(8,128)(2,1)S(1)}, bf16[64,8,8,512]{3,1,2,0:T(8,128)(2,1)}, u32[]{:S(2)}) copy-start(bf16[64,8,8,512]{3,1,2,0:T(8,128)(2,1)} %copy.29) | copy-start | bytes 12582916
  313.6 5.3 %collective-permute-start.10 = (bf16[128,1024]{1,0:T(8,128)(2,1)S(1)}, bf16[128,1024]{1,0:T(8,128)(2,1)S(1)}, u32[]{:S(2)}, u32[]{:S(2)}) collective-permute-start(bf16[128,1024]{1,0:T(8,128)(2,1)S(1)} %convolution_convert_fusion.2), channel_id=1, source_target_pairs={{0,1},{1,2},{2,3},{3,0},{4,5},{5,6},{6,7},{7,4},{8,9},{9,10},{10,1... | collective-permute-start | bytes 786440 | tf_op jit(solution)/shard_map/ppermute | solution.py:139
  313.6 12.0 %collective-permute-start.11 = (bf16[128,1024]{1,0:T(8,128)(2,1)S(1)}, bf16[128,1024]{1,0:T(8,128)(2,1)S(1)}, u32[]{:S(2)}, u32[]{:S(2)}) collective-permute-start(bf16[128,1024]{1,0:T(8,128)(2,1)S(1)} %convolution_convert_fusion.1), channel_id=1, source_target_pairs={{0,2},{1,3},{2,0},{3,1},{4,6},{5,7},{6,4},{7,5},{8,10},{9,11},{10,... | collective-permute-start | bytes 786440 | tf_op jit(solution)/shard_map/ppermute | solution.py:139
  316.7 11.8 %collective-permute-start.12 = (bf16[128,1024]{1,0:T(8,128)(2,1)S(1)}, bf16[128,1024]{1,0:T(8,128)(2,1)S(1)}, u32[]{:S(2)}, u32[]{:S(2)}) collective-permute-start(bf16[128,1024]{1,0:T(8,128)(2,1)S(1)} %convolution_convert_fusion), channel_id=1, source_target_pairs={{0,3},{1,0},{2,1},{3,2},{4,7},{5,4},{6,5},{7,6},{8,11},{9,8},{10,9... | collective-permute-start | bytes 786440 | tf_op jit(solution)/shard_map/ppermute | solution.py:139
  328.5 3.6 %copy-start.1 = (f32[2048,8]{0,1:T(8,128)S(1)}, f32[2048,8]{0,1:T(8,128)}, u32[]{:S(2)}) copy-start(f32[2048,8]{0,1:T(8,128)} %param.11) | copy-start | bytes 196612
Sparse Core Ops, SparseCore 0:
  9.9 91.4 all-gather.3
  104.6 93.0 all-gather.5
  200.2 55.9 all-gather.7

commit v6 on v4

--- a/solution.py
+++ b/solution.py
@@ -124,6 +124,8 @@
     span = rows.shape[0] // count
     parts = []
     for shift in list(range(1, count)) + [0]:
+        if not shift:
+            parts, rows = lax.optimization_barrier((parts, rows))
         target = lax.rem(me + shift, count)
         block_rows = lax.dynamic_slice_in_dim(rows, target * span, span, 0)
         parts.append(

time: 303 us -> 303 us (level)
  no operation moved by 1% of the time
where the time goes in v6:
time: 303 us; the launch traced here: 302 us
  waiting for transfers between devices  154 us (51%)
  matrix products  39.7 us (13%)
  Pallas kernels  30.5 us (10%)
  local copies, waits for them, and re-layouts  29.4 us (10%)
  other arithmetic  27.5 us (9%)
  between operations  14.1 us (5%)
  starting transfers between devices  7.44 us (2%)
    all_gather x1, waiting for transfers between devices, shards(): query_full = lax.all_gather(query_weight, 'req', axis=1, tiled=True)  93.4 us
    all_gather x2, waiting for transfers between devices, shards(): lax.all_gather(piece, 'req', axis=2, tiled=True)  39.2 us
    pallas_call x1, Pallas kernels, attend(): pl.pallas_call(functools.partial(attention_kernel, cache_blocks=cache_blo...  30.5 us
    ppermute x6, waiting for transfers between devices, exchange_finish(): lax.ppermute(part, axis, [(src, (src + shift) % count) for src in range(c...  19.8 us
    dot_general x8, matrix products, exchange_parts(): jnp.dot(block_rows, weight, preferred_element_type=jnp.float32)  18 us
    dot_general x1, matrix products, shards(): jnp.einsum('tc,ecn->etn', normed, query_full, preferred_element_type=jnp....  15.1 us
    unnamed x28, local copies, waits for them, and re-layouts  12.2 us
    transpose x1, local copies, waits for them, and re-layouts, shards(): jnp.einsum('tc,ecn->etn', normed, query_full, preferred_element_type=jnp....  9.29 us
  transfers between devices with their start and end apart: 10, of which 5 were waited for; matrix products, arithmetic and copies ran while one was open for 29% of the time, Pallas kernels for 10%

profile of v6, /device:TPU:11, one launch (start us, length us, event | category | flops | bytes accessed | tf_op | source)
XLA Modules:
  0.0 302.3 jit_solution(14078795220031198326)
XLA Ops:
  8.0 93.4 %all-gather.5.cloned.1.call-done = bf16[8,2048,512]{2,1,0:T(8,128)(2,1)} async-done(((bf16[8,256,512]{2,1,0:T(8,128)(2,1)}), bf16[8,2048,512]{2,1,0:T(8,128)(2,1)}) %all-gather.5.cloned.1.call-update) | async-done | bytes 16777232 | tf_op jit(solution)/shard_map/all_gather | solution.py:252
  101.5 3.1 %fusion.31 = (bf16[8,512,128]{2,1,0:T(8,128)(2,1)}, bf16[8,512,128]{2,1,0:T(8,128)(2,1)}) fusion(bf16[8,512,256]{2,1,0:T(8,128)(2,1)} %param.14), kind=kLoop, calls=%fused_computation.67 | loop fusion | bytes 4194304 | tf_op jit(solution)/shard_map/slice | solution.py:260
  107.0 1.8 fusion.29
  110.2 15.1 %convolution_bitcast_fusion = f32[8,512,512]{1,2,0:T(8,128)} fusion(bf16[8,2048,512]{2,1,0:T(8,128)(2,1)} %all-gather.5.cloned.1.call-done, bf16[512,2048]{1,0:T(8,128)(2,1)S(1)} %copy-done.6, f32[2048]{0:T(1024)S(1)} %copy-done.9, f32[512]{0:T(512)S(1)} %add_rsqrt_fusion), kind=kOutput, calls=%fused_computation.7 | convolution fusion | flops 8594128896 | bytes 27273216 | tf_op jit(solution)/shard_map/tc,ecn->etn/dot_general | solution.py:263
  125.2 9.3 %copy.25 = f32[8,512,512]{2,1,0:T(8,128)} copy(f32[8,512,512]{1,2,0:T(8,128)} %convolution_bitcast_fusion) | data formatting | bytes 16777216 | tf_op jit(solution)/shard_map/tc,ecn->etn/transpose | solution.py:263
  134.5 6.4 %select_reduce_fusion = f32[2,512,512]{2,1,0:T(8,128)} fusion(f32[8,512,512]{2,1,0:T(8,128)} %copy.25, pred[2,8,512]{2,1,0:T(8,128)(4,1)S(1)} %iota_compare_fusion.1), kind=kLoop, calls=%fused_computation | loop fusion | flops 7864320 | bytes 10493952 | tf_op jit(solution)/shard_map/reduce_sum | solution.py:275
  140.9 1.9 reshape.248
  142.8 1.7 subtract_convert_fusion
  144.6 1.4 pad_maximum_fusion
  147.2 4.9 %fusion.26 = f32[512,1024]{0,1:T(8,128)S(1)} fusion(bf16[2048,1024]{1,0:T(8,128)(2,1)} %all-gather.7.cloned.1.call-done, bf16[512,2048]{1,0:T(8,128)(2,1)S(1)} %copy-done.7, f32[2048]{0:T(1024)S(1)} %copy-done.9, f32[512]{0:T(512)S(1)} %add_rsqrt_fusion), kind=kOutput, calls=%fused_computation.65 | convolution fusion | flops 2151677952 | bytes 8398848 | tf_op jit(solution)/shard_map/dot_general | solution.py:262
  153.4 1.3 copy.33
  155.1 1.4 pad_maximum_fusion.1.fresh_ref
  156.6 30.5 %shard_map.104 = f32[1024,512]{1,0:T(8,128)} custom-call(s32[1]{0:T(128)} %bitcast.2.length_ref, bf16[1024,512]{1,0:T(8,128)(2,1)} %bitcast.82, bf16[4,2048,256]{2,1,0:T(8,128)(2,1)} %bitcast.87, bf16[4,512,256]{2,1,0:T(8,128)(2,1)} %pad_maximum_fusion.1.fresh_ref), custom_call_target="tpu_custom_call" | custom-call | flops 5368709120 | bytes 8388608 | tf_op jit(solution)/shard_map/pallas_call | solution.py:218
  187.1 1.8 multiply_convert_fusion
  188.9 8.6 %select_reduce_fusion.1 = bf16[512,8,512]{2,1,0:T(8,128)(2,1)S(1)} fusion(pred[2,512,8]{2,1,0:T(8,128)(4,1)S(1)} %iota_compare_fusion, bf16[2,512,512]{2,1,0:T(8,128)(2,1)S(1)} %multiply_convert_fusion), kind=kLoop, calls=%fused_computation.1 | loop fusion | flops 6291456 | bytes 5251072 | tf_op jit(solution)/shard_map/reduce_sum | solution.py:283
  197.5 4.2 %copy.35 = bf16[64,8,8,512]{3,1,2,0:T(8,128)(2,1)} copy(bf16[64,8,8,512]{3,2,1,0:T(8,128)(2,1)S(1)} %bitcast.72) | data formatting | bytes 8388608
  201.7 5.1 %convolution_convert_fusion.5 = bf16[128,1024]{1,0:T(8,128)(2,1)S(1)} fusion(bf16[4096,1024]{1,0:T(8,128)(2,1)} %bitcast.56, bf16[512,4096]{1,0:T(8,128)(2,1)} %bitcast.64, s32[]{:T(128)S(6)} %select_n.38), kind=kOutput, calls=%fused_computation.18 | convolution fusion | flops 1073872896 | bytes 9699332 | tf_op jit(solution)/shard_map/dot_general | solution.py:132
  208.1 1.6 copy-done.4
  209.7 1.3 convolution_convert_fusion.6
  211.0 1.3 convolution_convert_fusion.7
  212.3 1.3 collective-permute-start
  215.9 1.3 convolution_convert_fusion.4
  217.2 39.2 %all-gather.11.cloned.1.call-done = bf16[8,512,1024]{2,1,0:T(8,128)(2,1)} async-done(((bf16[8,512,128]{2,1,0:T(8,128)(2,1)}), bf16[8,512,1024]{2,1,0:T(8,128)(2,1)}) %all-gather.11.cloned.1.call-update) | async-done | bytes 8388624 | tf_op jit(solution)/shard_map/all_gather | solution.py:259
  256.3 5.1 %convolution_convert_fusion.1 = bf16[128,1024]{1,0:T(8,128)(2,1)S(1)} fusion(bf16[4096,1024]{1,0:T(8,128)(2,1)} %bitcast.60, bf16[512,4096]{1,0:T(8,128)(2,1)} %bitcast.65, s32[]{:T(128)S(6)} %select_n.38), kind=kOutput, calls=%fused_computation.14 | convolution fusion | flops 1073872896 | bytes 9699332 | tf_op jit(solution)/shard_map/dot_general | solution.py:132
  263.6 1.3 convolution_convert_fusion.2
  264.9 1.3 convolution_convert_fusion.3
  266.1 1.3 collective-permute-start.3
  269.8 1.4 pad_maximum_fusion.2
  272.4 1.5 collective-permute-done.3
  273.9 15.9 %collective-permute-done.4 = bf16[128,1024]{1,0:T(8,128)(2,1)S(1)} collective-permute-done((bf16[128,1024]{1,0:T(8,128)(2,1)S(1)}, bf16[128,1024]{1,0:T(8,128)(2,1)S(1)}, u32[]{:S(2)}, u32[]{:S(2)}) %collective-permute-start.4) | collective-permute-done | bytes 262176 | tf_op jit(solution)/shard_map/ppermute | solution.py:141
  289.7 2.5 collective-permute-done.5
  292.2 1.4 fusion.14
  (61 shorter events, 18.8 us)
Async XLA Ops:
  7.2 99.9 %copy-start = (f32[2048,8]{0,1:T(8,128)S(1)}, f32[2048,8]{0,1:T(8,128)}, u32[]{:S(2)}) copy-start(f32[2048,8]{0,1:T(8,128)} %param.11) | copy-start | bytes 196612
  7.2 98.0 %copy-start.10 = (s32[8]{0:T(128)S(1)}, s32[8]{0:T(128)}, u32[]{:S(2)}) copy-start(s32[8]{0:T(128)} %param.16) | copy-start | bytes 100
  7.2 99.3 %copy-start.6 = (bf16[512,2048]{1,0:T(8,128)(2,1)S(1)}, bf16[512,2048]{1,0:T(8,128)(2,1)}, u32[]{:S(2)}) copy-start(bf16[512,2048]{1,0:T(8,128)(2,1)} %param.9) | copy-start | bytes 6291460
  7.2 94.2 %all-gather.5.cloned.1.call-start = ((), (), s32[]{:S(2)}) async-start(), calls=%async_computation | async-start | bytes 18874368 | tf_op jit(solution)/shard_map/all_gather | solution.py:252
  7.9 139.2 %all-gather.7.cloned.1.call-start = ((), (), s32[]{:S(2)}) async-start(), calls=%async_computation.1 | async-start | bytes 4718592 | tf_op jit(solution)/shard_map/all_gather | solution.py:256
  101.4 5.6 %copy-start.9 = (f32[2048]{0:T(1024)S(1)}, f32[2048]{0:T(1024)}, u32[]{:S(2)}) copy-start(f32[2048]{0:T(1024)} %param.10) | copy-start | bytes 24580
  101.4 100.3 %all-gather.9.cloned.1.call-start = ((), (), s32[]{:S(2)}) async-start(), calls=%async_computation.2 | async-start | bytes 9437184 | tf_op jit(solution)/shard_map/all_gather | solution.py:259
  104.6 4.3 %copy-start.8 = (s32[512,2]{0,1:T(2,128)S(1)}, s32[512,2]{0,1:T(2,128)}, u32[]{:S(2)}) copy-start(s32[512,2]{0,1:T(2,128)} %param.15) | copy-start | bytes 12292
  104.6 151.7 %all-gather.11.cloned.1.call-start = ((), (), s32[]{:S(2)}) async-start(), calls=%async_computation.3 | async-start | bytes 9437184 | tf_op jit(solution)/shard_map/all_gather | solution.py:259
  144.6 2.6 copy-start.7
  201.7 6.4 %copy-start.2 = (bf16[8,512,1024]{2,1,0:T(8,128)(2,1)S(1)}, bf16[8,512,1024]{2,1,0:T(8,128)(2,1)}, u32[]{:S(2)}) copy-start(bf16[8,512,1024]{2,1,0:T(8,128)(2,1)} %all-gather.9.cloned.1.call-done) | copy-start | bytes 25165828
  201.7 8.0 %copy-start.4 = (bf16[64,8,8,512]{3,1,2,0:T(8,128)(2,1)S(1)}, bf16[64,8,8,512]{3,1,2,0:T(8,128)(2,1)}, u32[]{:S(2)}) copy-start(bf16[64,8,8,512]{3,1,2,0:T(8,128)(2,1)} %copy.35) | copy-start | bytes 12582916
  212.3 56.3 %collective-permute-start = (bf16[128,1024]{1,0:T(8,128)(2,1)S(1)}, bf16[128,1024]{1,0:T(8,128)(2,1)S(1)}, u32[]{:S(2)}, u32[]{:S(2)}) collective-permute-start(bf16[128,1024]{1,0:T(8,128)(2,1)S(1)} %convolution_convert_fusion.7), channel_id=1, source_target_pairs={{0,1},{1,2},{2,3},{3,0},{4,5},{5,6},{6,7},{7,4},{8,9},{9,10},{10,1... | collective-permute-start | bytes 786440 | tf_op jit(solution)/shard_map/ppermute | solution.py:141
  213.5 57.7 %collective-permute-start.1 = (bf16[128,1024]{1,0:T(8,128)(2,1)S(1)}, bf16[128,1024]{1,0:T(8,128)(2,1)S(1)}, u32[]{:S(2)}, u32[]{:S(2)}) collective-permute-start(bf16[128,1024]{1,0:T(8,128)(2,1)S(1)} %convolution_convert_fusion.6), channel_id=1, source_target_pairs={{0,2},{1,3},{2,0},{3,1},{4,6},{5,7},{6,4},{7,5},{8,10},{9,11},{10,... | collective-permute-start | bytes 786440 | tf_op jit(solution)/shard_map/ppermute | solution.py:141
  214.7 56.6 %collective-permute-start.2 = (bf16[128,1024]{1,0:T(8,128)(2,1)S(1)}, bf16[128,1024]{1,0:T(8,128)(2,1)}, u32[]{:S(2)}, u32[]{:S(2)}) collective-permute-start(bf16[128,1024]{1,0:T(8,128)(2,1)S(1)} %convolution_convert_fusion.5), channel_id=1, source_target_pairs={{0,3},{1,0},{2,1},{3,2},{4,7},{5,4},{6,5},{7,6},{8,11},{9,8},{10,9... | collective-permute-start | bytes 786440 | tf_op jit(solution)/shard_map/ppermute | solution.py:141
  256.3 6.1 %copy-start.3 = (bf16[8,512,1024]{2,1,0:T(8,128)(2,1)S(1)}, bf16[8,512,1024]{2,1,0:T(8,128)(2,1)}, u32[]{:S(2)}) copy-start(bf16[8,512,1024]{2,1,0:T(8,128)(2,1)} %all-gather.11.cloned.1.call-done) | copy-start | bytes 25165828
  256.3 7.3 %copy-start.5 = (bf16[64,8,8,512]{3,1,2,0:T(8,128)(2,1)S(1)}, bf16[64,8,8,512]{3,1,2,0:T(8,128)(2,1)}, u32[]{:S(2)}) copy-start(bf16[64,8,8,512]{3,1,2,0:T(8,128)(2,1)} %copy.35) | copy-start | bytes 12582916
  266.1 7.7 %collective-permute-start.3 = (bf16[128,1024]{1,0:T(8,128)(2,1)S(1)}, bf16[128,1024]{1,0:T(8,128)(2,1)S(1)}, u32[]{:S(2)}, u32[]{:S(2)}) collective-permute-start(bf16[128,1024]{1,0:T(8,128)(2,1)S(1)} %convolution_convert_fusion.3), channel_id=1, source_target_pairs={{0,1},{1,2},{2,3},{3,0},{4,5},{5,6},{6,7},{7,4},{8,9},{9,10},{10,1... | collective-permute-start | bytes 786440 | tf_op jit(solution)/shard_map/ppermute | solution.py:141
  267.4 22.3 %collective-permute-start.4 = (bf16[128,1024]{1,0:T(8,128)(2,1)S(1)}, bf16[128,1024]{1,0:T(8,128)(2,1)S(1)}, u32[]{:S(2)}, u32[]{:S(2)}) collective-permute-start(bf16[128,1024]{1,0:T(8,128)(2,1)S(1)} %convolution_convert_fusion.2), channel_id=1, source_target_pairs={{0,2},{1,3},{2,0},{3,1},{4,6},{5,7},{6,4},{7,5},{8,10},{9,11},{10,... | collective-permute-start | bytes 786440 | tf_op jit(solution)/shard_map/ppermute | solution.py:141
  268.5 23.7 %collective-permute-start.5 = (bf16[128,1024]{1,0:T(8,128)(2,1)S(1)}, bf16[128,1024]{1,0:T(8,128)(2,1)S(1)}, u32[]{:S(2)}, u32[]{:S(2)}) collective-permute-start(bf16[128,1024]{1,0:T(8,128)(2,1)S(1)} %convolution_convert_fusion.1), channel_id=1, source_target_pairs={{0,3},{1,0},{2,1},{3,2},{4,7},{5,4},{6,5},{7,6},{8,11},{9,8},{10,9... | collective-permute-start | bytes 786440 | tf_op jit(solution)/shard_map/ppermute | solution.py:141
  292.2 3.6 %copy-start.1 = (f32[2048,8]{0,1:T(8,128)S(1)}, f32[2048,8]{0,1:T(8,128)}, u32[]{:S(2)}) copy-start(f32[2048,8]{0,1:T(8,128)} %param.11) | copy-start | bytes 196612
Sparse Core Ops, SparseCore 0:
  9.9 91.4 all-gather.4
  103.3 36.7 all-gather.6
  141.9 55.9 all-gather.8
  200.2 56.0 all-gather.10
